TPU v7x, 128 devices: a whole 4x4x4 slice. The times are simulated.
128 devices in a mesh: group: 4 (over y), local: 32 (over x, z, core).
Axes of the slice: x: 4, y: 4, z: 4, core: 2. Of those that a mesh axis runs over, the one named last changes fastest.
Arguments:
- tokens: bfloat16 [16384, 3584], P(('group', 'local')), may hold values from -6 to 6
- grad_out: bfloat16 [16384, 3584], P(('group', 'local')), may hold values from -6 to 6
- expert_ids: int32 [16384, 4], P(('group', 'local')), may hold values from 0 to 127, as said below
- combine: bfloat16 [16384, 4], P(('group', 'local')), may hold values from 0.099609375 to 1
- gate_weight: bfloat16 [128, 3584, 1024], P(('group', 'local')), may hold values from -0.09375 to 0.09375
- up_weight: bfloat16 [128, 3584, 1024], P(('group', 'local')), may hold values from -0.09375 to 0.09375
- down_weight: bfloat16 [128, 1024, 3584], P(('group', 'local')), may hold values from -0.1875 to 0.1875
Outputs:
- grad_tokens: bfloat16 [16384, 3584], P(('group', 'local'))
- grad_combine: bfloat16 [16384, 4], P(('group', 'local'))
Inputs may be any that keep to these rules, and one draw needn't show every extreme that they name: `expert_ids`: each token names 4 different experts; expert e lies in node group e // 32. The first 2 experts of a token lie in one group and the other 2 in another, so a token uses 2 groups. The tokens of each device choose every group exactly 128//2 times. The tokens of one device name one expert at most 6 times, and in every draw some expert is named 6 times by the tokens of every device.
All inputs are finite; a program needn't handle non-finite values.
Results may differ from a plain program's by a relative error of at most 0.0058.
Values may be sent and summed in bfloat16 or wider, within the bound.
No kernel may reach another device: no remote copies, remote signals or barrier semaphores. Data moves between devices by JAX's collectives and lax.ppermute only.
A program may use at most 128 MiB of HBM per device.

v0:
```python
import jax
import jax.numpy as jnp
from jax import lax
from jax.sharding import PartitionSpec as P


def expert_rows(rows_x, rows_dy, rows_p, gate_mat, up_mat, down_mat):
    gate_pre = jnp.dot(rows_x, gate_mat, preferred_element_type=jnp.float32)
    up_pre = jnp.dot(rows_x, up_mat, preferred_element_type=jnp.float32)
    sigmoid_gate = jax.nn.sigmoid(gate_pre)
    active = gate_pre * sigmoid_gate
    hidden = (active * up_pre).astype(jnp.bfloat16)
    output = jnp.dot(hidden, down_mat, preferred_element_type=jnp.float32)
    grad_weight = jnp.sum(rows_dy.astype(jnp.float32) * output, axis=1).astype(jnp.bfloat16)
    back_hidden = lax.dot_general(
        rows_dy, down_mat, (((1,), (1,)), ((), ())), preferred_element_type=jnp.float32
    )
    back_hidden = back_hidden * rows_p.astype(jnp.float32)[:, None]
    grad_gate = (
        back_hidden * up_pre * sigmoid_gate * (1.0 + gate_pre * (1.0 - sigmoid_gate))
    ).astype(jnp.bfloat16)
    grad_up = (back_hidden * active).astype(jnp.bfloat16)
    contrib = lax.dot_general(
        grad_gate, gate_mat, (((1,), (1,)), ((), ())), preferred_element_type=jnp.float32
    )
    contrib = contrib + lax.dot_general(
        grad_up, up_mat, (((1,), (1,)), ((), ())), preferred_element_type=jnp.float32
    )
    return (contrib.astype(jnp.bfloat16), grad_weight)


def local(tokens, grad_out, expert_ids, combine, gate_weight, up_weight, down_weight):
    token_rows, model_width = tokens.shape
    top_count = expert_ids.shape[1]
    group_count = lax.axis_size("group")
    local_count = lax.axis_size("local")
    expert_count = group_count * local_count
    mean_pair = token_rows * top_count // expert_count
    pair_cap = mean_pair + (mean_pair + 1) // 2
    gate_mat = gate_weight[0]
    up_mat = up_weight[0]
    down_mat = down_weight[0]
    zero_value = jnp.zeros((), jnp.bfloat16)
    assign_count = token_rows * top_count
    targets = expert_ids.reshape(assign_count)
    one_hot = (targets[:, None] == jnp.arange(expert_count, dtype=jnp.int32)[None, :]).astype(
        jnp.int32
    )
    rank_in = jnp.sum((jnp.cumsum(one_hot, axis=0) - 1) * one_hot, axis=1)
    slot_of = targets * pair_cap + rank_in
    slot_total = expert_count * pair_cap
    owner = (
        jnp.full((slot_total,), assign_count, jnp.int32)
        .at[slot_of]
        .set(jnp.arange(assign_count, dtype=jnp.int32))
    )
    filled = owner < assign_count
    safe_owner = jnp.minimum(owner, assign_count - 1)
    token_of = safe_owner // top_count
    send_x = jnp.where(filled[:, None], tokens[token_of], zero_value).reshape(
        expert_count, pair_cap, model_width
    )
    send_dy = jnp.where(filled[:, None], grad_out[token_of], zero_value).reshape(
        expert_count, pair_cap, model_width
    )
    send_p = jnp.where(filled, combine.reshape(assign_count)[safe_owner], zero_value).reshape(
        expert_count, pair_cap
    )
    rows_x = lax.all_to_all(send_x, ("group", "local"), split_axis=0, concat_axis=0, tiled=True)
    rows_dy = lax.all_to_all(send_dy, ("group", "local"), split_axis=0, concat_axis=0, tiled=True)
    rows_p = lax.all_to_all(send_p, ("group", "local"), split_axis=0, concat_axis=0, tiled=True)
    leading = rows_x.shape[:2]
    contrib, grad_weight = expert_rows(
        rows_x.reshape(-1, model_width),
        rows_dy.reshape(-1, model_width),
        rows_p.reshape(-1),
        gate_mat,
        up_mat,
        down_mat,
    )
    contrib, grad_weight = (contrib.reshape(leading + (model_width,)), grad_weight.reshape(leading))
    back_rows = lax.all_to_all(contrib, ("group", "local"), split_axis=0, concat_axis=0, tiled=True)
    back_weight = lax.all_to_all(
        grad_weight, ("group", "local"), split_axis=0, concat_axis=0, tiled=True
    )
    back_rows = back_rows.reshape(slot_total, model_width)
    terms = back_rows[slot_of].reshape(token_rows, top_count, model_width)
    grad_tokens = jnp.sum(terms.astype(jnp.float32), axis=1).astype(jnp.bfloat16)
    grad_combine = back_weight.reshape(slot_total)[slot_of].reshape(token_rows, top_count)
    return (grad_tokens, grad_combine)


def solution(mesh):
    placed = (
        P(("group", "local"), None),
        P(("group", "local"), None),
        P(("group", "local"), None),
        P(("group", "local"), None),
        P(("group", "local"), None, None),
        P(("group", "local"), None, None),
        P(("group", "local"), None, None),
    )
    return jax.shard_map(
        local,
        mesh=mesh,
        in_specs=placed,
        out_specs=(P(("group", "local"), None), P(("group", "local"), None)),
        check_vma=False,
    )
```

profile of v0, /device:TPU:1, one launch (start us, length us, event | category | flops | bytes accessed | tf_op | source)
XLA Modules:
  0.0 469.5 jit_solution(11636345204522811347)
XLA Ops:
  0.6 0.0 copy-start
  0.6 0.8 broadcast_multiply_fusion
  1.4 0.8 copy.17
  2.2 0.1 eq.29
  2.3 0.1 eq.25
  2.4 0.8 copy.21
  3.2 0.1 reshape.121
  3.3 0.1 copy.16
  3.5 0.1 mul.53
  3.6 0.1 copy.19
  3.7 0.2 fusion.20
  3.9 0.1 add_add_fusion
  4.0 0.2 fusion.19
  4.3 0.0 copy-start.5
  4.3 2.4 scatter_custom_fusion
  6.8 0.0 copy-done.5
  6.8 5.0 %gather_fusion.1 = bf16[768]{0:T(1024)(128)(2,1)S(1)} fusion(bf16[512]{0:T(512)(128)(2,1)S(1)} %reshape.121, s32[1024]{0:T(1024)S(1)} %get-tuple-element.12), kind=kCustom, calls=%fused_computation.1 | custom fusion | bytes 6144 | tf_op jit(solution)/shard_map/gather | solution.py:66
  11.8 0.8 all_to_all.25
  12.6 11.5 %all-to-all-start.1 = ((bf16[128,1,6]{2,1,0:T(2,128)(2,1)}), bf16[128,1,6]{2,1,0:T(2,128)(2,1)S(1)}, u32[]{:S(2)}, u32[]{:S(2)}) async-start(bf16[128,1,6]{2,1,0:T(2,128)(2,1)} %all_to_all.25), calls=%async_computation.1 | async-start | bytes 131072 | tf_op jit(solution)/shard_map/all_to_all | solution.py:71
  24.1 0.2 broadcast_in_dim.36
  24.3 0.0 copy-done
  24.3 5.4 %gather_fusion.2 = bf16[768,3584]{1,0:T(8,128)(2,1)} fusion(bf16[128,3584]{1,0:T(8,128)(2,1)S(1)} %copy-done, s32[1024]{0:T(1024)S(1)} %get-tuple-element.13), kind=kCustom, calls=%fused_computation.2 | custom fusion | bytes 11013120 | tf_op jit(solution)/shard_map/gather | solution.py:60
  29.7 9.7 %gather.23 = bf16[128,6,3584]{2,1,0:T(8,128)(2,1)} reshape(bf16[768,3584]{1,0:T(8,128)(2,1)} %gather_fusion.2) | data formatting | bytes 11010048 | tf_op jit(solution)/shard_map/gather | solution.py:60
  39.4 0.0 copy-done.2
  39.4 5.4 %gather_fusion = bf16[768,3584]{1,0:T(8,128)(2,1)} fusion(bf16[128,3584]{1,0:T(8,128)(2,1)S(1)} %copy-done.2, s32[1024]{0:T(1024)S(1)} %get-tuple-element.13), kind=kCustom, calls=%fused_computation | custom fusion | bytes 11013120 | tf_op jit(solution)/shard_map/gather | solution.py:63
  44.8 9.6 %gather.20 = bf16[128,6,3584]{2,1,0:T(8,128)(2,1)} reshape(bf16[768,3584]{1,0:T(8,128)(2,1)} %gather_fusion) | data formatting | bytes 11010048 | tf_op jit(solution)/shard_map/gather | solution.py:63
  54.3 10.7 %broadcast_select_fusion.1 = (bf16[128,6,3584]{2,1,0:T(8,128)(2,1)}, bf16[128,6,3584]{2,1,0:T(8,128)(2,1)}) fusion(bf16[128,6,3584]{2,1,0:T(8,128)(2,1)} %gather.20, pred[128,6]{1,0:T(8,128)(4,1)S(1)} %broadcast_in_dim.36, bf16[128,6,3584]{2,1,0:T(8,128)(2,1)} %gather.23), kind=kLoop, calls=%fused_computation.20 | loop fusion | flops 5505024 | bytes 22020864 | tf_op jit(solution)/shard_map/jit(_where)/select_n | solution.py:63
  65.0 0.0 all-to-all-done.1
  65.0 96.2 %all_to_all.31 = bf16[128,6,3584]{2,1,0:T(8,128)(2,1)} all-to-all(bf16[128,6,3584]{2,1,0:T(8,128)(2,1)} %get-tuple-element.9), channel_id=1, replica_groups=mesh['group'=4,'local'=32] {'group','local'}, dimensions={0} | all-to-all | bytes 11010048 | tf_op jit(solution)/shard_map/all_to_all | solution.py:69
  161.3 5.9 %all-to-all-start = ((bf16[128,6,3584]{2,1,0:T(8,128)(2,1)}), bf16[128,6,3584]{2,1,0:T(8,128)(2,1)}, u32[]{:S(2)}, u32[]{:S(2)}) async-start(bf16[128,6,3584]{2,1,0:T(8,128)(2,1)} %get-tuple-element.8), calls=%async_computation | async-start | bytes 14680064 | tf_op jit(solution)/shard_map/all_to_all | solution.py:70
  167.2 0.2 convert_reduce_fusion
  167.4 0.1 reshape.128
  167.5 9.7 %reshape.122 = bf16[768,3584]{1,0:T(8,128)(2,1)} reshape(bf16[128,6,3584]{2,1,0:T(8,128)(2,1)} %all_to_all.31) | data formatting | bytes 11010048 | tf_op jit(solution)/shard_map/reshape | solution.py:74
  177.2 11.9 %fusion.2 = f32[768,1024]{1,0:T(8,128)} fusion(bf16[768,3584]{1,0:T(8,128)(2,1)} %reshape.122, bf16[1,3584,1024]{2,1,0:T(8,128)(2,1)} %param.11), kind=kOutput, calls=%fused_computation.10 | convolution fusion | flops 5637144576 | bytes 15990784 | tf_op jit(solution)/shard_map/dot_general | solution.py:8
  189.1 0.0 copy-done.3
  189.1 9.2 %fusion.6 = f32[768,1024]{1,0:T(8,128)} fusion(bf16[768,3584]{1,0:T(8,128)(2,1)S(1)} %copy-done.3, bf16[1,3584,1024]{2,1,0:T(8,128)(2,1)} %param.12), kind=kOutput, calls=%fused_computation.14 | convolution fusion | flops 5637144576 | bytes 15990784 | tf_op jit(solution)/shard_map/dot_general | solution.py:9
  198.3 58.8 %all-to-all-done = bf16[128,6,3584]{2,1,0:T(8,128)(2,1)} async-done(((bf16[128,6,3584]{2,1,0:T(8,128)(2,1)}), bf16[128,6,3584]{2,1,0:T(8,128)(2,1)}, u32[]{:S(2)}, u32[]{:S(2)}) %all-to-all-start) | async-done | bytes 5505056 | tf_op jit(solution)/shard_map/all_to_all | solution.py:70
  257.1 9.7 %reshape.120 = bf16[768,3584]{1,0:T(8,128)(2,1)} reshape(bf16[128,6,3584]{2,1,0:T(8,128)(2,1)} %all-to-all-done) | data formatting | bytes 11010048 | tf_op jit(solution)/shard_map/reshape | solution.py:75
  266.7 11.1 %fusion.9 = f32[768,1024]{1,0:T(8,128)} fusion(bf16[768,3584]{1,0:T(8,128)(2,1)} %reshape.120, bf16[1,1024,3584]{2,1,0:T(8,128)(2,1)} %param.13), kind=kOutput, calls=%fused_computation.17 | convolution fusion | flops 5637144576 | bytes 15990784 | tf_op jit(solution)/shard_map/dot_general | solution.py:15
  277.8 0.0 copy-done.4
  277.8 0.0 copy-done.7
  277.8 0.0 copy-done.10
  277.8 9.6 %multiply_reduce_fusion = bf16[768]{0:T(1024)(128)(2,1)S(1)} fusion(bf16[768,3584]{1,0:T(8,128)(2,1)S(1)} %copy-done.4, bf16[1,1024,3584]{2,1,0:T(8,128)(2,1)} %param.13, f32[768,1024]{1,0:T(8,128)S(1)} %copy-done.10, f32[768,1024]{1,0:T(8,128)S(1)} %copy-done.7), kind=kOutput, calls=%fused_computation.6 | convolution fusion | flops 5650119680 | bytes 19138048 | tf_op jit(solution)/shard_map/dot_general | solution.py:13
  287.5 0.8 convert_element_type.57
  288.3 7.0 %all-to-all-start.4 = ((bf16[128,1,6]{2,1,0:T(2,128)(2,1)}), bf16[128,1,6]{2,1,0:T(2,128)(2,1)S(1)}, u32[]{:S(2)}, u32[]{:S(2)}) async-start(bf16[128,1,6]{2,1,0:T(2,128)(2,1)} %convert_element_type.57), calls=%async_computation.4 | async-start | bytes 131072 | tf_op jit(solution)/shard_map/all_to_all | solution.py:83
  295.3 0.0 copy-start.8
  295.3 0.0 copy-start.9
  295.3 16.1 %fusion = f32[768,3584]{1,0:T(8,128)} fusion(bf16[1,3584,1024]{2,1,0:T(8,128)(2,1)} %param.11, f32[768,1024]{1,0:T(8,128)} %fusion.2, f32[768,1024]{1,0:T(8,128)} %fusion.6, f32[768,1024]{1,0:T(8,128)} %fusion.9, f32[768]{0:T(1024)S(1)} %reshape.128), kind=kOutput, calls=%fused_computation.8 | convolution fusion | flops 5645795328 | bytes 27790336 | tf_op jit(solution)/shard_map/dot_general | solution.py:23
  311.4 0.0 copy-done.8
  311.4 0.0 copy-done.9
  311.4 13.2 %add_convert_fusion = bf16[768,3584]{1,0:T(8,128)(2,1)} fusion(f32[768,3584]{1,0:T(8,128)} %fusion, bf16[1,3584,1024]{2,1,0:T(8,128)(2,1)} %param.12, f32[768,1024]{1,0:T(8,128)S(1)} %copy-done.9, f32[768]{0:T(1024)S(1)} %reshape.128, f32[768,1024]{1,0:T(8,128)S(1)} %copy-done.8), kind=kOutput, calls=%fused_computation.7 | convolution fusion | flops 5648154624 | bytes 30149632 | tf_op jit(solution)/shard_map/dot_general | solution.py:26
  324.6 9.6 %reshape.123 = bf16[128,6,3584]{2,1,0:T(8,128)(2,1)} reshape(bf16[768,3584]{1,0:T(8,128)(2,1)} %add_convert_fusion) | data formatting | bytes 11010048 | tf_op jit(solution)/shard_map/reshape | solution.py:81
  334.2 0.0 all-to-all-done.4
  334.2 10.2 %all-to-all-start.3 = ((bf16[128,6,3584]{2,1,0:T(8,128)(2,1)}), bf16[128,6,3584]{2,1,0:T(8,128)(2,1)}, u32[]{:S(2)}, u32[]{:S(2)}) async-start(bf16[128,6,3584]{2,1,0:T(8,128)(2,1)} %reshape.123), calls=%async_computation.3 | async-start | bytes 14680064 | tf_op jit(solution)/shard_map/all_to_all | solution.py:82
  344.4 0.2 reduce.2
  344.6 0.1 reshape.126
  344.7 3.5 gather_fusion.4
  348.3 0.1 reshape.127
  348.4 0.7 copy.24
  349.0 85.1 %all-to-all-done.3 = bf16[128,6,3584]{2,1,0:T(8,128)(2,1)} async-done(((bf16[128,6,3584]{2,1,0:T(8,128)(2,1)}), bf16[128,6,3584]{2,1,0:T(8,128)(2,1)}, u32[]{:S(2)}, u32[]{:S(2)}) %all-to-all-start.3) | async-done | bytes 5505056 | tf_op jit(solution)/shard_map/all_to_all | solution.py:82
  434.1 9.7 %reshape.124 = bf16[768,3584]{1,0:T(8,128)(2,1)} reshape(bf16[128,6,3584]{2,1,0:T(8,128)(2,1)} %all-to-all-done.3) | data formatting | bytes 11010048 | tf_op jit(solution)/shard_map/reshape | solution.py:86
  443.8 11.2 %gather_fusion.3 = bf16[512,3584]{1,0:T(8,128)(2,1)} fusion(bf16[768,3584]{1,0:T(8,128)(2,1)} %reshape.124, s32[1024]{0:T(1024)S(1)} %pad_clamp_fusion), kind=kCustom, calls=%fused_computation.3 | custom fusion | bytes 7342080 | tf_op jit(solution)/shard_map/gather | solution.py:87
  455.0 7.0 %reshape.125 = bf16[128,4,3584]{2,1,0:T(4,128)(2,1)} reshape(bf16[512,3584]{1,0:T(8,128)(2,1)} %gather_fusion.3) | data formatting | bytes 7340032 | tf_op jit(solution)/shard_map/reshape | solution.py:87
  462.0 7.4 %reduce_sum.34 = bf16[128,3584]{1,0:T(8,128)(2,1)} reduce(bf16[128,4,3584]{2,1,0:T(4,128)(2,1)} %reshape.125, bf16[]{:T(256)} %constant.39.clone.1), dimensions={1}, to_apply=%region_4.5 | reduce | flops 1376256 | bytes 4587522 | tf_op jit(solution)/shard_map/reduce_sum | solution.py:88
  (19 shorter events, 0.1 us)
Async XLA Ops:
  0.6 23.7 %copy-start = (bf16[128,3584]{1,0:T(8,128)(2,1)S(1)}, bf16[128,3584]{1,0:T(8,128)(2,1)}, u32[]{:S(2)}) copy-start(bf16[128,3584]{1,0:T(8,128)(2,1)} %param.7) | copy-start | bytes 2752516
  4.3 2.5 copy-start.5
  12.6 52.4 %all-to-all-start.1 = ((bf16[128,1,6]{2,1,0:T(2,128)(2,1)}), bf16[128,1,6]{2,1,0:T(2,128)(2,1)S(1)}, u32[]{:S(2)}, u32[]{:S(2)}) async-start(bf16[128,1,6]{2,1,0:T(2,128)(2,1)} %all_to_all.25), calls=%async_computation.1 | async-start | bytes 131072 | tf_op jit(solution)/shard_map/all_to_all | solution.py:71
  29.7 9.7 %copy-start.2 = (bf16[128,3584]{1,0:T(8,128)(2,1)S(1)}, bf16[128,3584]{1,0:T(8,128)(2,1)}, u32[]{:S(2)}) copy-start(bf16[128,3584]{1,0:T(8,128)(2,1)} %param.8) | copy-start | bytes 2752516
  161.3 95.8 %all-to-all-start = ((bf16[128,6,3584]{2,1,0:T(8,128)(2,1)}), bf16[128,6,3584]{2,1,0:T(8,128)(2,1)}, u32[]{:S(2)}, u32[]{:S(2)}) async-start(bf16[128,6,3584]{2,1,0:T(8,128)(2,1)} %get-tuple-element.8), calls=%async_computation | async-start | bytes 14680064 | tf_op jit(solution)/shard_map/all_to_all | solution.py:70
  177.2 11.9 %copy-start.3 = (bf16[768,3584]{1,0:T(8,128)(2,1)S(1)}, bf16[768,3584]{1,0:T(8,128)(2,1)}, u32[]{:S(2)}) copy-start(bf16[768,3584]{1,0:T(8,128)(2,1)} %reshape.122) | copy-start | bytes 16515076
  266.7 11.1 %copy-start.4 = (bf16[768,3584]{1,0:T(8,128)(2,1)S(1)}, bf16[768,3584]{1,0:T(8,128)(2,1)}, u32[]{:S(2)}) copy-start(bf16[768,3584]{1,0:T(8,128)(2,1)} %reshape.120) | copy-start | bytes 16515076
  266.7 11.1 %copy-start.7 = (f32[768,1024]{1,0:T(8,128)S(1)}, f32[768,1024]{1,0:T(8,128)}, u32[]{:S(2)}) copy-start(f32[768,1024]{1,0:T(8,128)} %fusion.2) | copy-start | bytes 9437188
  266.7 11.1 %copy-start.10 = (f32[768,1024]{1,0:T(8,128)S(1)}, f32[768,1024]{1,0:T(8,128)}, u32[]{:S(2)}) copy-start(f32[768,1024]{1,0:T(8,128)} %fusion.6) | copy-start | bytes 9437188
  288.3 45.9 %all-to-all-start.4 = ((bf16[128,1,6]{2,1,0:T(2,128)(2,1)}), bf16[128,1,6]{2,1,0:T(2,128)(2,1)S(1)}, u32[]{:S(2)}, u32[]{:S(2)}) async-start(bf16[128,1,6]{2,1,0:T(2,128)(2,1)} %convert_element_type.57), calls=%async_computation.4 | async-start | bytes 131072 | tf_op jit(solution)/shard_map/all_to_all | solution.py:83
  295.3 16.1 %copy-start.8 = (f32[768,1024]{1,0:T(8,128)S(1)}, f32[768,1024]{1,0:T(8,128)}, u32[]{:S(2)}) copy-start(f32[768,1024]{1,0:T(8,128)} %fusion.2) | copy-start | bytes 9437188
  295.3 16.1 %copy-start.9 = (f32[768,1024]{1,0:T(8,128)S(1)}, f32[768,1024]{1,0:T(8,128)}, u32[]{:S(2)}) copy-start(f32[768,1024]{1,0:T(8,128)} %fusion.9) | copy-start | bytes 9437188
  334.2 10.2 %copy-start.6 = (s32[512,1]{0,1:T(1,128)S(1)}, s32[512,1]{0,1:T(1,128)}, u32[]{:S(2)}) copy-start(s32[512,1]{0,1:T(1,128)} %copy-done.5) | copy-start | bytes 6148
  334.2 99.9 %all-to-all-start.3 = ((bf16[128,6,3584]{2,1,0:T(8,128)(2,1)}), bf16[128,6,3584]{2,1,0:T(8,128)(2,1)}, u32[]{:S(2)}, u32[]{:S(2)}) async-start(bf16[128,6,3584]{2,1,0:T(8,128)(2,1)} %reshape.123), calls=%async_computation.3 | async-start | bytes 14680064 | tf_op jit(solution)/shard_map/all_to_all | solution.py:82
  443.8 25.7 %copy-start.1 = (bf16[128,3584]{1,0:T(8,128)(2,1)S(1)}, bf16[128,3584]{1,0:T(8,128)(2,1)}, u32[]{:S(2)}) copy-start(bf16[128,3584]{1,0:T(8,128)(2,1)} %param.7) | copy-start | bytes 2752516
where the time goes:
time: 471 us; the launch traced here: 469 us
  waiting for transfers between devices  144 us (31%)
  local copies, waits for them, and re-layouts  103 us (22%)
  blocking collectives  96.2 us (20%)
  matrix products  71.1 us (15%)
  starting transfers between devices  34.6 us (7%)
  other arithmetic  19.8 us (4%)
    all_to_all x1, blocking collectives, local(): lax.all_to_all(send_x, ('group', 'local'), split_axis=0, concat_axis=0, t...  96.2 us
    all_to_all x1, waiting for transfers between devices, local(): lax.all_to_all(contrib, ('group', 'local'), split_axis=0, concat_axis=0,...  85.1 us
    all_to_all x1, waiting for transfers between devices, local(): lax.all_to_all(send_dy, ('group', 'local'), split_axis=0, concat_axis=0,...  58.8 us
    dot_general x1, matrix products, expert_rows(): lax.dot_general(grad_gate, gate_mat, (((1,), (1,)), ((), ())), preferred_...  16.1 us
    gather x2, local copies, waits for them, and re-layouts, local(): tokens[token_of]  15.1 us
    gather x2, local copies, waits for them, and re-layouts, local(): grad_out[token_of]  14.9 us
    dot_general x1, matrix products, expert_rows(): lax.dot_general(grad_up, up_mat, (((1,), (1,)), ((), ())), preferred_elem...  13.2 us
    dot_general x1, matrix products, expert_rows(): gate_pre = jnp.dot(rows_x, gate_mat, preferred_element_type=jnp.float32)  11.9 us
  transfers between devices with their start and end apart: 4, of which 2 were waited for; matrix products, arithmetic and copies ran while one was open for 25% of the time, Pallas kernels for 0%

commit v1 on v0

v1 whole, which is shorter than its diff:
```python
import jax
import jax.numpy as jnp
from jax import lax
from jax.sharding import PartitionSpec as P


def _t_dot(a, b):
    return lax.dot_general(a, b, (((1,), (1,)), ((), ())), preferred_element_type=jnp.float32)


def local(tokens, grad_out, expert_ids, combine, gate_weight, up_weight, down_weight):
    token_rows, model_width = tokens.shape
    top_count = expert_ids.shape[1]
    group_count = lax.axis_size("group")
    local_count = lax.axis_size("local")
    expert_count = group_count * local_count
    mean_pair = token_rows * top_count // expert_count
    pair_cap = mean_pair + (mean_pair + 1) // 2
    slot_cap = (pair_cap + 7) // 8 * 8
    gate_mat = gate_weight[0]
    up_mat = up_weight[0]
    down_mat = down_weight[0]
    ff = gate_mat.shape[1]
    assign_count = token_rows * top_count
    lane = 128
    targets = expert_ids.reshape(assign_count)
    one_hot = (targets[:, None] == jnp.arange(expert_count, dtype=jnp.int32)[None, :]).astype(
        jnp.int32
    )
    rank_in = jnp.sum((jnp.cumsum(one_hot, axis=0) - 1) * one_hot, axis=1)
    slot_of = targets * slot_cap + rank_in
    slot_total = expert_count * slot_cap
    sel = slot_of[None, :] == jnp.arange(slot_total, dtype=jnp.int32)[:, None]
    sel_a = sel.astype(jnp.bfloat16)
    sel_t = jnp.any(sel.reshape(slot_total, token_rows, top_count), axis=2).astype(jnp.bfloat16)

    send_x = jnp.dot(sel_t, tokens, preferred_element_type=jnp.bfloat16)
    p_block = jnp.zeros((assign_count, lane), jnp.bfloat16).at[:, 0].set(combine.reshape(assign_count))
    dy_rep = jnp.broadcast_to(grad_out[:, None, :], (token_rows, top_count, model_width)).reshape(
        assign_count, model_width
    )
    send_dyp = jnp.dot(
        sel_a, jnp.concatenate([dy_rep, p_block], axis=1), preferred_element_type=jnp.bfloat16
    )

    def a2a(v):
        v = v.reshape(expert_count, slot_cap, v.shape[-1])
        v = lax.all_to_all(v, ("group", "local"), split_axis=0, concat_axis=0, tiled=True)
        return v.reshape(slot_total, v.shape[-1])

    rows_x = a2a(send_x)
    gate_pre = jnp.dot(rows_x, gate_mat, preferred_element_type=jnp.float32)
    up_pre = jnp.dot(rows_x, up_mat, preferred_element_type=jnp.float32)
    sigmoid_gate = jax.nn.sigmoid(gate_pre)
    active = gate_pre * sigmoid_gate
    hidden = (active * up_pre).astype(jnp.bfloat16)
    output = jnp.dot(hidden, down_mat, preferred_element_type=jnp.float32)

    rows_dyp = a2a(send_dyp)
    rows_dy = rows_dyp[:, :model_width]
    rows_p = rows_dyp[:, model_width]
    grad_weight = jnp.sum(rows_dy.astype(jnp.float32) * output, axis=1).astype(jnp.bfloat16)
    back_hidden = _t_dot(rows_dy, down_mat)
    back_hidden = back_hidden * rows_p.astype(jnp.float32)[:, None]
    grad_gate = (
        back_hidden * up_pre * sigmoid_gate * (1.0 + gate_pre * (1.0 - sigmoid_gate))
    ).astype(jnp.bfloat16)
    grad_up = (back_hidden * active).astype(jnp.bfloat16)

    half = model_width // 2
    contrib_a = (_t_dot(grad_gate, gate_mat[:half]) + _t_dot(grad_up, up_mat[:half])).astype(
        jnp.bfloat16
    )
    gw_block = jnp.zeros((slot_total, lane), jnp.bfloat16).at[:, 0].set(grad_weight)
    back_a = a2a(jnp.concatenate([contrib_a, gw_block], axis=1))
    contrib_b = (_t_dot(grad_gate, gate_mat[half:]) + _t_dot(grad_up, up_mat[half:])).astype(
        jnp.bfloat16
    )
    back_b = a2a(contrib_b)

    sum_a = jnp.dot(sel_t.T, back_a[:, :half], preferred_element_type=jnp.float32)
    sum_b = jnp.dot(sel_t.T, back_b, preferred_element_type=jnp.float32)
    grad_tokens = jnp.concatenate([sum_a, sum_b], axis=1).astype(jnp.bfloat16)
    gw_back = jnp.dot(sel_a.T, back_a[:, half:], preferred_element_type=jnp.float32)
    grad_combine = gw_back[:, 0].astype(jnp.bfloat16).reshape(token_rows, top_count)
    return (grad_tokens, grad_combine)


def solution(mesh):
    placed = (
        P(("group", "local"), None),
        P(("group", "local"), None),
        P(("group", "local"), None),
        P(("group", "local"), None),
        P(("group", "local"), None, None),
        P(("group", "local"), None, None),
        P(("group", "local"), None, None),
    )
    return jax.shard_map(
        local,
        mesh=mesh,
        in_specs=placed,
        out_specs=(P(("group", "local"), None), P(("group", "local"), None)),
        check_vma=False,
    )
```

time: 471 us -> 362 us (0.77)
  blocking collectives: 96.2 us -> 0 us
  local copies, waits for them, and re-layouts: 103 us -> 12.3 us
  waiting for transfers between devices: 144 us -> 200 us
  matrix products: 71.1 us -> 105 us
  other arithmetic: 19.8 us -> 7.66 us
    all_to_all x1 -> x0, blocking collectives: 96.2 us -> none  [local(): lax.all_to_all(send_x, ('group', 'local'), split_axis=0, concat_axis=0, t...]
    all_to_all x4, waiting for transfers between devices: 144 us -> 200 us  [a2a(): lax.all_to_all(v, ('group', 'local'), split_axis=0, concat_axis=0, tiled=...]
    gather x7 -> x0, local copies, waits for them, and re-layouts: 49.8 us -> none  [the longest x2 15.1 us: local(): tokens[token_of]]
    reshape x8 -> x1, local copies, waits for them, and re-layouts: 46 us -> 6.75 us  [local(): jnp.broadcast_to(grad_out[:, None, :], (token_rows, top_count, model_width))]
    dot_general x6 -> x13, matrix products: 71.1 us -> 105 us  [the longest x5 43.1 us: _t_dot(): lax.dot_general(a, b, (((1,), (1,)), ((), ())), preferred_element_type=jn...]
    select_n x4 -> x0, other arithmetic: 10.7 us -> none  [the longest x1 10.7 us: local(): jnp.where(filled[:, None], grad_out[token_of], zero_value)]
    reduce_sum x1 -> x0, other arithmetic: 7.42 us -> none  [local(): jnp.sum(terms.astype(jnp.float32), axis=1).astype(jnp.bfloat16)]
  transfers between devices with their start and end apart: 4 -> 4, of which waited for: 2 -> 4; matrix products, arithmetic and copies ran while one was open for 25% -> 22% of each run, Pallas kernels for 0% -> 0%
where the time goes in v1:
time: 362 us; the launch traced here: 361 us
  waiting for transfers between devices  200 us (55%)
  matrix products  105 us (29%)
  starting transfers between devices  35.3 us (10%)
  local copies, waits for them, and re-layouts  12.3 us (3%)
  other arithmetic  7.66 us (2%)
    all_to_all x4, waiting for transfers between devices, a2a(): lax.all_to_all(v, ('group', 'local'), split_axis=0, concat_axis=0, tiled=...  200 us
    dot_general x5, matrix products, _t_dot(): lax.dot_general(a, b, (((1,), (1,)), ((), ())), preferred_element_type=jn...  43.1 us
    all_to_all x4, starting transfers between devices, a2a(): lax.all_to_all(v, ('group', 'local'), split_axis=0, concat_axis=0, tiled=...  35.3 us
    dot_general x1, matrix products, local(): output = jnp.dot(hidden, down_mat, preferred_element_type=jnp.float32)  14.9 us
    dot_general x1, matrix products, local(): gate_pre = jnp.dot(rows_x, gate_mat, preferred_element_type=jnp.float32)  13.5 us
    dot_general x1, matrix products, local(): up_pre = jnp.dot(rows_x, up_mat, preferred_element_type=jnp.float32)  13.4 us
    dot_general x1, matrix products, local(): jnp.dot(sel_a, jnp.concatenate([dy_rep, p_block], axis=1), preferred_elem...  8.39 us
  transfers between devices with their start and end apart: 4, of which 4 were waited for; matrix products, arithmetic and copies ran while one was open for 22% of the time, Pallas kernels for 0%

profile of v1, /device:TPU:1, one launch (start us, length us, event | category | flops | bytes accessed | tf_op | source)
XLA Modules:
  0.0 360.9 jit_solution(11400957028598683085)
XLA Ops:
  0.6 0.0 copy-start
  0.6 0.9 copy.48
  1.5 0.1 eq.45
  1.6 0.1 eq.49
  1.7 0.1 copy.50
  1.8 0.2 fusion.54
  2.1 0.1 add_add_fusion
  2.2 0.2 fusion.53
  2.4 0.1 reduce_sum.21
  2.6 0.1 copy.52
  2.6 0.7 multiply_add_fusion.1
  3.3 0.4 fusion.44
  3.7 0.0 copy-done
  3.7 5.0 %fusion.48 = bf16[128,8,3584]{2,1,0:T(8,128)(2,1)} fusion(bf16[128,3584]{1,0:T(8,128)(2,1)S(1)} %copy-done, pred[1024,128]{1,0:T(8,128)(4,1)S(1)} %fusion.44), kind=kOutput, calls=%fused_computation.54 | convolution fusion | flops 939524096 | bytes 8388608 | tf_op jit(solution)/shard_map/dot_general | solution.py:37
  8.7 0.0 copy-start.3
  8.7 0.0 copy-start.2
  8.7 11.9 %all-to-all-start.1 = ((bf16[128,8,3584]{2,1,0:T(8,128)(2,1)}), bf16[128,8,3584]{2,1,0:T(8,128)(2,1)}, u32[]{:S(2)}, u32[]{:S(2)}) async-start(bf16[128,8,3584]{2,1,0:T(8,128)(2,1)} %fusion.48), calls=%async_computation.1 | async-start | bytes 14680064 | tf_op jit(solution)/shard_map/all_to_all | solution.py:48
  20.6 0.6 compare_reduce_fusion
  21.2 0.0 copy-done.3
  21.3 0.6 broadcast_select_fusion
  21.9 0.1 copy.53
  22.0 0.1 reshape.169
  22.2 0.0 copy-done.2
  22.2 2.9 broadcast_in_dim.2
  25.0 6.7 %reshape.156 = bf16[512,3584]{1,0:T(8,128)(2,1)} reshape(bf16[128,4,3584]{2,1,0:T(4,128)(2,1)} %broadcast_in_dim.2) | data formatting | bytes 7340032 | tf_op jit(solution)/shard_map/reshape | solution.py:39
  31.8 8.4 %convolution_bitcast_fusion = bf16[128,8,3712]{2,1,0:T(8,128)(2,1)} fusion(bf16[512,1]{1,0:T(8,128)(2,1)S(1)} %reshape.169, bf16[512,3584]{1,0:T(8,128)(2,1)} %reshape.156, s32[512]{0:T(512)S(1)} %multiply_add_fusion), kind=kOutput, calls=%fused_computation.16 | convolution fusion | flops 3904241664 | bytes 11275264 | tf_op jit(solution)/shard_map/dot_general | solution.py:42
  40.2 70.2 %all-to-all-done.1 = bf16[128,8,3584]{2,1,0:T(8,128)(2,1)} async-done(((bf16[128,8,3584]{2,1,0:T(8,128)(2,1)}), bf16[128,8,3584]{2,1,0:T(8,128)(2,1)}, u32[]{:S(2)}, u32[]{:S(2)}) %all-to-all-start.1) | async-done | bytes 7340064 | tf_op jit(solution)/shard_map/all_to_all | solution.py:48
  110.4 7.3 %all-to-all-start = ((bf16[128,8,3712]{2,1,0:T(8,128)(2,1)}), bf16[128,8,3712]{2,1,0:T(8,128)(2,1)}, u32[]{:S(2)}, u32[]{:S(2)}) async-start(bf16[128,8,3712]{2,1,0:T(8,128)(2,1)} %convolution_bitcast_fusion), calls=%async_computation | async-start | bytes 15204352 | tf_op jit(solution)/shard_map/all_to_all | solution.py:48
  117.7 13.5 %fusion.2 = f32[1024,1024]{1,0:T(8,128)} fusion(bf16[1,3584,1024]{2,1,0:T(8,128)(2,1)} %param.15, bf16[128,8,3584]{2,1,0:T(8,128)(2,1)} %all-to-all-done.1), kind=kOutput, calls=%fused_computation.5 | convolution fusion | flops 7516192768 | bytes 18874368 | tf_op jit(solution)/shard_map/dot_general | solution.py:52
  131.2 13.4 %fusion.4 = f32[1024,1024]{1,0:T(8,128)} fusion(bf16[1,3584,1024]{2,1,0:T(8,128)(2,1)} %param.16, bf16[128,8,3584]{2,1,0:T(8,128)(2,1)} %all-to-all-done.1), kind=kOutput, calls=%fused_computation.7 | convolution fusion | flops 7516192768 | bytes 18874368 | tf_op jit(solution)/shard_map/dot_general | solution.py:53
  144.6 65.7 %all-to-all-done = bf16[128,8,3712]{2,1,0:T(8,128)(2,1)} async-done(((bf16[128,8,3712]{2,1,0:T(8,128)(2,1)}), bf16[128,8,3712]{2,1,0:T(8,128)(2,1)}, u32[]{:S(2)}, u32[]{:S(2)}) %all-to-all-start) | async-done | bytes 7602208 | tf_op jit(solution)/shard_map/all_to_all | solution.py:48
  210.3 1.1 convert_reduce_fusion
  211.4 15.4 %multiply_convert_fusion.1 = (bf16[1024,1024]{1,0:T(8,128)(2,1)S(1)}, bf16[1024,1024]{1,0:T(8,128)(2,1)S(1)}) fusion(f32[1024]{0:T(1024)S(1)} %convert_reduce_fusion, f32[1024,1024]{1,0:T(8,128)} %fusion.2, f32[1024,1024]{1,0:T(8,128)} %fusion.4, bf16[1,1024,3584]{2,1,0:T(8,128)(2,1)} %param.17, bf16[1024,3712]{1,0:T(8,128)(2,1)} %bitcast.4), kind=kOutput, calls=%fused_computation.19 | convolution fusion | flops 7530872832 | bytes 27267072 | tf_op jit(solution)/shard_map/dot_general | solution.py:8
  226.8 0.0 copy-start.4
  226.8 0.0 copy-start.6
  226.8 7.5 %fusion.25 = f32[1024,1792]{1,0:T(8,128)S(1)} fusion(bf16[1024,1024]{1,0:T(8,128)(2,1)S(1)} %get-tuple-element.37, bf16[1,3584,1024]{2,1,0:T(8,128)(2,1)} %param.15), kind=kOutput, calls=%fused_computation.34 | convolution fusion | flops 3758096384 | bytes 13107200 | tf_op jit(solution)/shard_map/dot_general | solution.py:8
  234.4 0.0 copy-done.4
  234.4 0.0 copy-done.6
  234.4 7.6 %fusion.34 = bf16[128,8,1792]{2,1,0:T(8,128)(2,1)} fusion(f32[1024,1792]{1,0:T(8,128)S(1)} %fusion.25, bf16[1024,1024]{1,0:T(8,128)(2,1)S(1)} %get-tuple-element.36, bf16[1,3584,1024]{2,1,0:T(8,128)(2,1)} %param.16), kind=kOutput, calls=%fused_computation.43 | convolution fusion | flops 3761766400 | bytes 16777216 | tf_op jit(solution)/shard_map/dot_general | solution.py:8
  242.0 10.2 %all-to-all-start.3 = ((bf16[128,8,1792]{2,1,0:T(8,128)(2,1)}), bf16[128,8,1792]{2,1,0:T(8,128)(2,1)}, u32[]{:S(2)}, u32[]{:S(2)}) async-start(bf16[128,8,1792]{2,1,0:T(8,128)(2,1)} %fusion.34), calls=%async_computation.3 | async-start | bytes 7340032 | tf_op jit(solution)/shard_map/all_to_all | solution.py:48
  252.3 0.0 copy-start.5
  252.3 14.9 %multiply_reduce_fusion = bf16[1024]{0:T(1024)(128)(2,1)S(1)} fusion(bf16[1,1024,3584]{2,1,0:T(8,128)(2,1)} %param.17, bf16[1024,3712]{1,0:T(8,128)(2,1)} %bitcast.4, f32[1024,1024]{1,0:T(8,128)} %fusion.4, f32[1024,1024]{1,0:T(8,128)} %fusion.2), kind=kOutput, calls=%fused_computation | convolution fusion | flops 7533493248 | bytes 23070720 | tf_op jit(solution)/shard_map/dot_general | solution.py:57
  267.2 0.7 convert_select_fusion
  267.8 0.2 reshape.168
  268.0 0.0 copy-done.5
  268.0 0.0 copy-start.7
  268.0 6.2 %fusion.28 = f32[1024,1792]{1,0:T(8,128)S(1)} fusion(bf16[1024,1024]{1,0:T(8,128)(2,1)S(1)} %copy-done.5, bf16[1,3584,1024]{2,1,0:T(8,128)(2,1)} %param.15), kind=kOutput, calls=%fused_computation.37 | convolution fusion | flops 3758096384 | bytes 13107200 | tf_op jit(solution)/shard_map/dot_general | solution.py:8
  274.2 0.0 copy-done.7
  274.2 6.4 %add_convert_fusion.1 = bf16[1024,1792]{1,0:T(8,128)(2,1)S(1)} fusion(f32[1024,1792]{1,0:T(8,128)S(1)} %fusion.28, bf16[1024,1024]{1,0:T(8,128)(2,1)S(1)} %copy-done.7, bf16[1,3584,1024]{2,1,0:T(8,128)(2,1)} %param.16), kind=kOutput, calls=%fused_computation.15 | convolution fusion | flops 3761766400 | bytes 16777216 | tf_op jit(solution)/shard_map/dot_general | solution.py:8
  280.6 2.0 fusion.14
  282.7 16.3 %all-to-all-done.3 = bf16[128,8,1792]{2,1,0:T(8,128)(2,1)} async-done(((bf16[128,8,1792]{2,1,0:T(8,128)(2,1)}), bf16[128,8,1792]{2,1,0:T(8,128)(2,1)}, u32[]{:S(2)}, u32[]{:S(2)}) %all-to-all-start.3) | async-done | bytes 3670048 | tf_op jit(solution)/shard_map/all_to_all | solution.py:48
  299.0 5.8 %all-to-all-start.2 = ((bf16[128,8,1920]{2,1,0:T(8,128)(2,1)}), bf16[128,8,1920]{2,1,0:T(8,128)(2,1)}, u32[]{:S(2)}, u32[]{:S(2)}) async-start(bf16[128,8,1920]{2,1,0:T(8,128)(2,1)} %fusion.14), calls=%async_computation.2 | async-start | bytes 7864320 | tf_op jit(solution)/shard_map/all_to_all | solution.py:48
  304.8 2.7 fusion.37
  307.6 47.2 %all-to-all-done.2 = bf16[128,8,1920]{2,1,0:T(8,128)(2,1)} async-done(((bf16[128,8,1920]{2,1,0:T(8,128)(2,1)}), bf16[128,8,1920]{2,1,0:T(8,128)(2,1)}, u32[]{:S(2)}, u32[]{:S(2)}) %all-to-all-start.2) | async-done | bytes 3932192 | tf_op jit(solution)/shard_map/all_to_all | solution.py:48
  354.8 0.0 copy-start.1
  354.8 1.5 fusion.43
  356.4 2.7 fusion.40
  359.1 0.1 convert_element_type.50
  359.3 0.7 copy.58
  359.9 1.0 pad_maximum_fusion
  360.9 0.0 copy-done.1
  (6 shorter events, 0.1 us)
Async XLA Ops:
  0.6 3.1 copy-start
  8.7 12.6 %copy-start.3 = (bf16[128,4]{0,1:T(4,128)(2,1)S(1)}, bf16[128,4]{0,1:T(4,128)(2,1)}, u32[]{:S(2)}) copy-start(bf16[128,4]{0,1:T(4,128)(2,1)} %param.14) | copy-start | bytes 3076
  8.7 13.5 %copy-start.2 = (bf16[128,3584]{1,0:T(8,128)(2,1)S(1)}, bf16[128,3584]{1,0:T(8,128)(2,1)}, u32[]{:S(2)}) copy-start(bf16[128,3584]{1,0:T(8,128)(2,1)} %param.12) | copy-start | bytes 2752516
  8.7 101.7 %all-to-all-start.1 = ((bf16[128,8,3584]{2,1,0:T(8,128)(2,1)}), bf16[128,8,3584]{2,1,0:T(8,128)(2,1)}, u32[]{:S(2)}, u32[]{:S(2)}) async-start(bf16[128,8,3584]{2,1,0:T(8,128)(2,1)} %fusion.48), calls=%async_computation.1 | async-start | bytes 14680064 | tf_op jit(solution)/shard_map/all_to_all | solution.py:48
  110.4 100.0 %all-to-all-start = ((bf16[128,8,3712]{2,1,0:T(8,128)(2,1)}), bf16[128,8,3712]{2,1,0:T(8,128)(2,1)}, u32[]{:S(2)}, u32[]{:S(2)}) async-start(bf16[128,8,3712]{2,1,0:T(8,128)(2,1)} %convolution_bitcast_fusion), calls=%async_computation | async-start | bytes 15204352 | tf_op jit(solution)/shard_map/all_to_all | solution.py:48
  226.8 7.6 %copy-start.4 = (bf16[1024,1024]{1,0:T(8,128)(2,1)}, bf16[1024,1024]{1,0:T(8,128)(2,1)S(1)}, u32[]{:S(2)}) copy-start(bf16[1024,1024]{1,0:T(8,128)(2,1)S(1)} %get-tuple-element.37) | copy-start | bytes 6291460
  226.8 7.6 %copy-start.6 = (bf16[1024,1024]{1,0:T(8,128)(2,1)}, bf16[1024,1024]{1,0:T(8,128)(2,1)S(1)}, u32[]{:S(2)}) copy-start(bf16[1024,1024]{1,0:T(8,128)(2,1)S(1)} %get-tuple-element.36) | copy-start | bytes 6291460
  242.0 57.0 %all-to-all-start.3 = ((bf16[128,8,1792]{2,1,0:T(8,128)(2,1)}), bf16[128,8,1792]{2,1,0:T(8,128)(2,1)}, u32[]{:S(2)}, u32[]{:S(2)}) async-start(bf16[128,8,1792]{2,1,0:T(8,128)(2,1)} %fusion.34), calls=%async_computation.3 | async-start | bytes 7340032 | tf_op jit(solution)/shard_map/all_to_all | solution.py:48
  252.3 15.8 %copy-start.5 = (bf16[1024,1024]{1,0:T(8,128)(2,1)S(1)}, bf16[1024,1024]{1,0:T(8,128)(2,1)}, u32[]{:S(2)}) copy-start(bf16[1024,1024]{1,0:T(8,128)(2,1)} %copy-done.4) | copy-start | bytes 6291460
  268.0 6.2 %copy-start.7 = (bf16[1024,1024]{1,0:T(8,128)(2,1)S(1)}, bf16[1024,1024]{1,0:T(8,128)(2,1)}, u32[]{:S(2)}) copy-start(bf16[1024,1024]{1,0:T(8,128)(2,1)} %copy-done.6) | copy-start | bytes 6291460
  299.0 55.8 %all-to-all-start.2 = ((bf16[128,8,1920]{2,1,0:T(8,128)(2,1)}), bf16[128,8,1920]{2,1,0:T(8,128)(2,1)}, u32[]{:S(2)}, u32[]{:S(2)}) async-start(bf16[128,8,1920]{2,1,0:T(8,128)(2,1)} %fusion.14), calls=%async_computation.2 | async-start | bytes 7864320 | tf_op jit(solution)/shard_map/all_to_all | solution.py:48
  354.8 6.1 %copy-start.1 = (bf16[128,3584]{1,0:T(8,128)(2,1)S(1)}, bf16[128,3584]{1,0:T(8,128)(2,1)}, u32[]{:S(2)}) copy-start(bf16[128,3584]{1,0:T(8,128)(2,1)} %param.11) | copy-start | bytes 2752516

commit v2 on v1

v2 whole, which is shorter than its diff:
```python
import jax
import jax.numpy as jnp
from jax import lax
from jax.sharding import PartitionSpec as P


def _t_dot(a, b):
    return lax.dot_general(a, b, (((1,), (1,)), ((), ())), preferred_element_type=jnp.float32)


def _rank(keys, count):
    hot = (keys[:, None] == jnp.arange(count, dtype=jnp.int32)[None, :]).astype(jnp.int32)
    return jnp.sum((jnp.cumsum(hot, axis=0) - 1) * hot, axis=1)


def _pick(slots, total):
    return slots[None, :] == jnp.arange(total, dtype=jnp.int32)[:, None]


def local(tokens, grad_out, expert_ids, combine, gate_weight, up_weight, down_weight):
    token_rows, model_width = tokens.shape
    top_count = expert_ids.shape[1]
    group_count = lax.axis_size("group")
    local_count = lax.axis_size("local")
    expert_count = group_count * local_count
    mean_pair = token_rows * top_count // expert_count
    pair_cap = mean_pair + (mean_pair + 1) // 2
    per_half = top_count // 2
    n_pairs = token_rows * 2
    per_group = n_pairs // group_count
    cap2 = group_count * pair_cap
    slots2 = local_count * cap2
    lane = 128
    blk = (local_count + per_half + lane - 1) // lane * lane
    wide = 2 * model_width
    gate_mat = gate_weight[0]
    up_mat = up_weight[0]
    down_mat = down_weight[0]
    l_me = lax.axis_index("local")
    bf = jnp.bfloat16

    halves = expert_ids.reshape(n_pairs, per_half)
    pair_group = halves[:, 0] // local_count
    pair_loc = halves % local_count
    pair_comb = combine.reshape(n_pairs, per_half)
    slot1 = pair_group * per_group + _rank(pair_group, group_count)
    sel1 = _pick(slot1, n_pairs).astype(bf)
    cols = jnp.arange(blk, dtype=jnp.int32)
    cvec = jnp.sum(
        jnp.where(pair_loc[:, :, None] == cols[None, None, :], pair_comb[:, :, None], 0.0), axis=1
    )
    for j in range(per_half):
        cvec = jnp.where(cols[None, :] == local_count + j, pair_loc[:, j : j + 1].astype(jnp.float32), cvec)
    rep = lambda v: jnp.broadcast_to(v[:, None, :], (token_rows, 2, v.shape[-1])).reshape(n_pairs, -1)
    payload1 = jnp.concatenate([rep(tokens), rep(grad_out), cvec.astype(bf)], axis=1)
    send1 = jnp.dot(sel1, payload1, preferred_element_type=bf)
    recv1 = lax.all_to_all(
        send1.reshape(group_count, per_group, -1), "group", 0, 0, tiled=True
    ).reshape(n_pairs, -1)

    loc_q = recv1[:, wide + local_count : wide + local_count + per_half].astype(jnp.int32).reshape(-1)
    slot2 = loc_q * cap2 + _rank(loc_q, local_count)
    sel2_q = _pick(slot2, slots2)
    sel2 = jnp.any(sel2_q.reshape(slots2, n_pairs, per_half), axis=2).astype(bf)

    def a2a_local(v):
        v = v.reshape(local_count, cap2, v.shape[-1])
        v = lax.all_to_all(v, "local", 0, 0, tiled=True)
        return v.reshape(slots2, v.shape[-1])

    rows_x = a2a_local(jnp.dot(sel2, recv1[:, :model_width], preferred_element_type=bf))
    rows_dyp = a2a_local(jnp.dot(sel2, recv1[:, model_width:], preferred_element_type=bf))

    gate_pre = jnp.dot(rows_x, gate_mat, preferred_element_type=jnp.float32)
    up_pre = jnp.dot(rows_x, up_mat, preferred_element_type=jnp.float32)
    sigmoid_gate = jax.nn.sigmoid(gate_pre)
    active = gate_pre * sigmoid_gate
    hidden = (active * up_pre).astype(bf)
    output = jnp.dot(hidden, down_mat, preferred_element_type=jnp.float32)
    rows_dy = rows_dyp[:, :model_width]
    mine = (cols == l_me).astype(jnp.float32)
    rows_p = jnp.sum(rows_dyp[:, model_width:].astype(jnp.float32) * mine[None, :], axis=1)
    grad_weight = jnp.sum(rows_dy.astype(jnp.float32) * output, axis=1).astype(bf)
    back_hidden = _t_dot(rows_dy, down_mat)
    back_hidden = back_hidden * rows_p[:, None]
    grad_gate = (
        back_hidden * up_pre * sigmoid_gate * (1.0 + gate_pre * (1.0 - sigmoid_gate))
    ).astype(bf)
    grad_up = (back_hidden * active).astype(bf)

    half = model_width // 2
    contrib_a = (_t_dot(grad_gate, gate_mat[:half]) + _t_dot(grad_up, up_mat[:half])).astype(bf)
    gw_block = jnp.zeros((slots2, lane), bf).at[:, 0].set(grad_weight)
    back_a = a2a_local(jnp.concatenate([contrib_a, gw_block], axis=1))
    contrib_b = (_t_dot(grad_gate, gate_mat[half:]) + _t_dot(grad_up, up_mat[half:])).astype(bf)
    back_b = a2a_local(contrib_b)

    sum_a = jnp.dot(sel2.T, back_a[:, :half], preferred_element_type=jnp.float32)
    sum_b = jnp.dot(sel2.T, back_b, preferred_element_type=jnp.float32)
    gw_q = jnp.dot(sel2_q.astype(bf).T, back_a[:, half:], preferred_element_type=jnp.float32)
    gw_pair = gw_q[:, 0].reshape(n_pairs, per_half)
    gw_blk = jnp.zeros((n_pairs, lane), jnp.float32).at[:, :per_half].set(gw_pair)
    back1 = jnp.concatenate([sum_a, sum_b, gw_blk], axis=1).astype(bf)
    recv_b1 = lax.all_to_all(
        back1.reshape(group_count, per_group, -1), "group", 0, 0, tiled=True
    ).reshape(n_pairs, -1)

    sel1_t = jnp.any(
        sel1.astype(jnp.bool_).reshape(n_pairs, token_rows, 2), axis=2
    ).astype(bf)
    grad_tokens = jnp.dot(
        sel1_t.T, recv_b1[:, :model_width], preferred_element_type=jnp.float32
    ).astype(bf)
    gw_back = jnp.dot(sel1.T, recv_b1[:, model_width:], preferred_element_type=jnp.float32)
    grad_combine = gw_back[:, :per_half].astype(bf).reshape(token_rows, top_count)
    return (grad_tokens, grad_combine)


def solution(mesh):
    placed = (
        P(("group", "local"), None),
        P(("group", "local"), None),
        P(("group", "local"), None),
        P(("group", "local"), None),
        P(("group", "local"), None, None),
        P(("group", "local"), None, None),
        P(("group", "local"), None, None),
    )
    return jax.shard_map(
        local,
        mesh=mesh,
        in_specs=placed,
        out_specs=(P(("group", "local"), None), P(("group", "local"), None)),
        check_vma=False,
    )
```

time: 362 us -> 393 us (1.086)
  blocking collectives: 0 us -> 47.5 us
  matrix products: 105 us -> 88.4 us
  waiting for transfers between devices: 200 us -> 188 us
  other arithmetic: 7.66 us -> 12.6 us
  starting transfers between devices: 35.3 us -> 39.4 us
    all_to_all x0 -> x1, blocking collectives: none -> 47.5 us  [local(): lax.all_to_all(send1.reshape(group_count, per_group, -1), 'group', 0, 0,...]
    dot_general x5, matrix products: 43.1 us -> 31.2 us  [_t_dot(): lax.dot_general(a, b, (((1,), (1,)), ((), ())), preferred_element_type=jn...]
    all_to_all x4 -> x5, waiting for transfers between devices: 200 us -> 188 us  [the longest x4 165 us: a2a_local(): v = lax.all_to_all(v, 'local', 0, 0, tiled=True)]
    all_to_all x4 -> x5, starting transfers between devices: 35.3 us -> 39.4 us  [the longest x4 35.9 us: a2a_local(): v = lax.all_to_all(v, 'local', 0, 0, tiled=True)]
    unnamed x18 -> x23, local copies, waits for them, and re-layouts: 1.56 us -> 5.7 us
    dot_general x5 -> x8, matrix products: 20.4 us -> 22.5 us  [the longest x1 5.75 us: local(): jnp.dot(sel2, recv1[:, model_width:], preferred_element_type=bf)]
  transfers between devices with their start and end apart: 4 -> 5, of which waited for: 4 -> 5; matrix products, arithmetic and copies ran while one was open for 22% -> 12% of each run, Pallas kernels for 0% -> 0%
where the time goes in v2:
time: 393 us; the launch traced here: 392 us
  waiting for transfers between devices  188 us (48%)
  matrix products  88.4 us (22%)
  blocking collectives  47.5 us (12%)
  starting transfers between devices  39.4 us (10%)
  local copies, waits for them, and re-layouts  14.8 us (4%)
  other arithmetic  12.6 us (3%)
    all_to_all x4, waiting for transfers between devices, a2a_local(): v = lax.all_to_all(v, 'local', 0, 0, tiled=True)  165 us
    all_to_all x1, blocking collectives, local(): lax.all_to_all(send1.reshape(group_count, per_group, -1), 'group', 0, 0,...  47.5 us
    all_to_all x4, starting transfers between devices, a2a_local(): v = lax.all_to_all(v, 'local', 0, 0, tiled=True)  35.9 us
    dot_general x5, matrix products, _t_dot(): lax.dot_general(a, b, (((1,), (1,)), ((), ())), preferred_element_type=jn...  31.2 us
    all_to_all x1, waiting for transfers between devices, local(): lax.all_to_all(back1.reshape(group_count, per_group, -1), 'group', 0, 0,...  23 us
    dot_general x1, matrix products, local(): gate_pre = jnp.dot(rows_x, gate_mat, preferred_element_type=jnp.float32)  12.2 us
    dot_general x1, matrix products, local(): output = jnp.dot(hidden, down_mat, preferred_element_type=jnp.float32)  11.6 us
    dot_general x1, matrix products, local(): up_pre = jnp.dot(rows_x, up_mat, preferred_element_type=jnp.float32)  10.9 us
  transfers between devices with their start and end apart: 5, of which 5 were waited for; matrix products, arithmetic and copies ran while one was open for 12% of the time, Pallas kernels for 0%

profile of v2, /device:TPU:1, one launch (start us, length us, event | category | flops | bytes accessed | tf_op | source)
XLA Modules:
  0.0 391.6 jit_solution(8240080819193381951)
XLA Ops:
  0.6 0.8 copy.45
  1.5 0.2 slice_reduce_fusion
  1.8 0.2 fusion.54
  2.1 1.2 reduce-window.14
  3.4 0.1 copy.46
  3.5 0.1 copy.47
  3.7 0.8 copy.50
  4.7 2.2 broadcast_in_dim.78
  6.9 1.7 reshape.272
  8.6 0.9 broadcast_in_dim.54
  9.6 1.7 reshape.271
  11.2 0.2 fusion.52
  11.5 0.1 select_convert_fusion
  11.6 3.2 fusion.9
  14.8 47.5 %all_to_all.30 = bf16[4,64,7296]{2,1,0:T(8,128)(2,1)S(1)} all-to-all(bf16[4,64,7296]{2,1,0:T(8,128)(2,1)S(1)} %bitcast.104), channel_id=1, replica_groups=mesh['group'=4,'local'=32] {'group'}, dimensions={0} | all-to-all | bytes 7471104 | tf_op jit(solution)/shard_map/all_to_all | solution.py:57
  62.3 1.8 copy-done
  64.2 0.1 eq.158
  64.4 0.1 eq.162
  64.5 1.2 reduce-window.16
  65.7 0.2 slice_reduce_fusion.1
  66.0 0.1 fusion.62
  66.1 0.1 reduce_sum.56
  66.2 0.9 multiply_add_fusion
  67.3 0.3 fusion.38
  67.6 5.5 %fusion.37 = bf16[32,24,3584]{2,1,0:T(8,128)(2,1)} fusion(pred[32,24,256]{2,1,0:T(8,128)(4,1)S(1)} %bitcast.105, bf16[256,7296]{1,0:T(8,128)(2,1)} %bitcast.100), kind=kOutput, calls=%fused_computation.47 | convolution fusion | flops 1409286144 | bytes 7536640 | tf_op jit(solution)/shard_map/dot_general | solution.py:71
  73.0 10.1 %all-to-all-start.2 = ((bf16[32,24,3584]{2,1,0:T(8,128)(2,1)}), bf16[32,24,3584]{2,1,0:T(8,128)(2,1)}, u32[]{:S(2)}, u32[]{:S(2)}) async-start(bf16[32,24,3584]{2,1,0:T(8,128)(2,1)} %fusion.37), calls=%async_computation.2 | async-start | bytes 11010048 | tf_op jit(solution)/shard_map/all_to_all | solution.py:68
  83.2 5.7 %fusion.35 = bf16[32,24,3712]{2,1,0:T(8,128)(2,1)} fusion(pred[32,24,256]{2,1,0:T(8,128)(4,1)S(1)} %bitcast.106, bf16[256,7296]{1,0:T(8,128)(2,1)} %bitcast.101), kind=kOutput, calls=%fused_computation.43 | convolution fusion | flops 1459617792 | bytes 7798784 | tf_op jit(solution)/shard_map/dot_general | solution.py:72
  88.9 62.4 %all-to-all-done.2 = bf16[32,24,3584]{2,1,0:T(8,128)(2,1)} async-done(((bf16[32,24,3584]{2,1,0:T(8,128)(2,1)}), bf16[32,24,3584]{2,1,0:T(8,128)(2,1)}, u32[]{:S(2)}, u32[]{:S(2)}) %all-to-all-start.2) | async-done | bytes 5505056 | tf_op jit(solution)/shard_map/all_to_all | solution.py:68
  151.3 10.6 %all-to-all-start.1 = ((bf16[32,24,3712]{2,1,0:T(8,128)(2,1)}), bf16[32,24,3712]{2,1,0:T(8,128)(2,1)}, u32[]{:S(2)}, u32[]{:S(2)}) async-start(bf16[32,24,3712]{2,1,0:T(8,128)(2,1)} %fusion.35), calls=%async_computation.1 | async-start | bytes 11403264 | tf_op jit(solution)/shard_map/all_to_all | solution.py:68
  161.9 0.6 compare_reduce_fusion.2
  162.5 10.9 %fusion.2 = f32[768,1024]{1,0:T(8,128)} fusion(bf16[768,3584]{1,0:T(8,128)(2,1)} %bitcast.12, bf16[1,3584,1024]{2,1,0:T(8,128)(2,1)} %param.16), kind=kOutput, calls=%fused_computation.3 | convolution fusion | flops 5637144576 | bytes 15990784 | tf_op jit(solution)/shard_map/dot_general | solution.py:75
  173.4 58.9 %all-to-all-done.1 = bf16[32,24,3712]{2,1,0:T(8,128)(2,1)} async-done(((bf16[32,24,3712]{2,1,0:T(8,128)(2,1)}), bf16[32,24,3712]{2,1,0:T(8,128)(2,1)}, u32[]{:S(2)}, u32[]{:S(2)}) %all-to-all-start.1) | async-done | bytes 5701664 | tf_op jit(solution)/shard_map/all_to_all | solution.py:68
  232.3 9.9 %fusion.5 = f32[768,1024]{1,0:T(8,128)S(1)} fusion(bf16[1,1024,3584]{2,1,0:T(8,128)(2,1)} %param.17, bf16[768,3712]{1,0:T(8,128)(2,1)} %bitcast.9), kind=kOutput, calls=%fused_computation.6 | convolution fusion | flops 5637144576 | bytes 15990784 | tf_op jit(solution)/shard_map/dot_general | solution.py:8
  242.3 1.1 multiply_reduce_fusion.1
  243.4 12.2 %multiply_convert_fusion.2 = (bf16[768,1024]{1,0:T(8,128)(2,1)S(1)}, bf16[768,1024]{1,0:T(8,128)(2,1)S(1)}, f32[768,1024]{1,0:T(8,128)}) fusion(f32[768,1024]{1,0:T(8,128)S(1)} %copy-done.7, f32[768,1024]{1,0:T(8,128)S(1)} %fusion.5, f32[768]{0:T(1024)S(1)} %multiply_reduce_fusion.1, bf16[768,3584]{1,0:T(8,128)(2,1)} %bitcast.12, ...), kind=kOutput, calls=%fused_computation.34 | convolution fusion | flops 5648154624 | bytes 25431040 | tf_op jit(solution)/shard_map/dot_general | solution.py:74
  255.6 6.2 %fusion.15 = f32[768,1792]{1,0:T(8,128)S(1)} fusion(bf16[768,1024]{1,0:T(8,128)(2,1)S(1)} %get-tuple-element.39, bf16[1,3584,1024]{2,1,0:T(8,128)(2,1)} %param.16), kind=kOutput, calls=%fused_computation.20 | convolution fusion | flops 2818572288 | bytes 10747904 | tf_op jit(solution)/shard_map/dot_general | solution.py:8
  261.9 4.4 %add_convert_fusion = bf16[768,1792]{1,0:T(8,128)(2,1)} fusion(f32[768,1792]{1,0:T(8,128)S(1)} %fusion.15, bf16[768,1024]{1,0:T(8,128)(2,1)S(1)} %get-tuple-element.38, bf16[1,3584,1024]{2,1,0:T(8,128)(2,1)S(1)} %bitcast.118), kind=kOutput, calls=%fused_computation.10 | convolution fusion | flops 2821324800 | bytes 13500416 | tf_op jit(solution)/shard_map/dot_general | solution.py:8
  266.3 10.5 %all-to-all-start.4 = ((bf16[32,24,1792]{2,1,0:T(8,128)(2,1)}), bf16[32,24,1792]{2,1,0:T(8,128)(2,1)S(1)}, u32[]{:S(2)}, u32[]{:S(2)}) async-start(bf16[32,24,1792]{2,1,0:T(8,128)(2,1)} %bitcast.111), calls=%async_computation.4 | async-start | bytes 5505024 | tf_op jit(solution)/shard_map/all_to_all | solution.py:68
  276.7 11.6 %multiply_reduce_fusion = bf16[768]{0:T(1024)(128)(2,1)S(1)} fusion(bf16[1,1024,3584]{2,1,0:T(8,128)(2,1)} %param.17, bf16[768,3712]{1,0:T(8,128)(2,1)} %bitcast.9, f32[768,1024]{1,0:T(8,128)} %fusion.2, f32[768,1024]{1,0:T(8,128)} %get-tuple-element.40), kind=kOutput, calls=%fused_computation | convolution fusion | flops 5650119680 | bytes 19138048 | tf_op jit(solution)/shard_map/dot_general | solution.py:79
  288.4 0.7 convert_select_fusion
  289.0 0.2 reshape.290
  289.2 5.2 %fusion.19 = f32[768,1792]{1,0:T(8,128)S(1)} fusion(bf16[768,1024]{1,0:T(8,128)(2,1)S(1)} %copy-done.4, bf16[1,3584,1024]{2,1,0:T(8,128)(2,1)} %param.16), kind=kOutput, calls=%fused_computation.24 | convolution fusion | flops 2818572288 | bytes 10747904 | tf_op jit(solution)/shard_map/dot_general | solution.py:8
  294.5 5.4 %add_convert_fusion.1 = bf16[768,1792]{1,0:T(8,128)(2,1)S(1)} fusion(f32[768,1792]{1,0:T(8,128)S(1)} %fusion.19, bf16[768,1024]{1,0:T(8,128)(2,1)S(1)} %copy-done.6, bf16[1,3584,1024]{2,1,0:T(8,128)(2,1)} %param.15), kind=kOutput, calls=%fused_computation.11 | convolution fusion | flops 2821324800 | bytes 13500416 | tf_op jit(solution)/shard_map/dot_general | solution.py:8
  299.9 1.8 fusion.32
  301.7 10.3 %all-to-all-done.4 = bf16[32,24,1792]{2,1,0:T(8,128)(2,1)S(1)} async-done(((bf16[32,24,1792]{2,1,0:T(8,128)(2,1)}), bf16[32,24,1792]{2,1,0:T(8,128)(2,1)S(1)}, u32[]{:S(2)}, u32[]{:S(2)}) %all-to-all-start.4) | async-done | bytes 2752544 | tf_op jit(solution)/shard_map/all_to_all | solution.py:68
  312.0 1.6 copy-done.1
  313.6 4.7 %all-to-all-start.3 = ((bf16[32,24,1920]{2,1,0:T(8,128)(2,1)}), bf16[32,24,1920]{2,1,0:T(8,128)(2,1)S(1)}, u32[]{:S(2)}, u32[]{:S(2)}) async-start(bf16[32,24,1920]{2,1,0:T(8,128)(2,1)} %bitcast.17), calls=%async_computation.3 | async-start | bytes 5898240 | tf_op jit(solution)/shard_map/all_to_all | solution.py:68
  318.3 0.6 compare_reduce_fusion.1
  318.9 0.3 copy.54
  319.2 3.6 convolution_convert_fusion.1
  322.8 33.2 %all-to-all-done.3 = bf16[32,24,1920]{2,1,0:T(8,128)(2,1)S(1)} async-done(((bf16[32,24,1920]{2,1,0:T(8,128)(2,1)}), bf16[32,24,1920]{2,1,0:T(8,128)(2,1)S(1)}, u32[]{:S(2)}, u32[]{:S(2)}) %all-to-all-start.3) | async-done | bytes 2949152 | tf_op jit(solution)/shard_map/all_to_all | solution.py:68
  356.0 1.8 fusion.34
  357.9 1.0 fusion.42
  358.9 0.2 reshape.283
  359.1 2.9 pad_maximum_fusion
  362.0 3.6 all-to-all-start.5
  365.6 0.1 reduce_sum.53
  365.7 0.1 squeeze.14
  366.0 23.0 %all-to-all-done.5 = bf16[4,64,3712]{2,1,0:T(8,128)(2,1)S(1)} async-done(((bf16[4,64,3712]{2,1,0:T(8,128)(2,1)}), bf16[4,64,3712]{2,1,0:T(8,128)(2,1)S(1)}, u32[]{:S(2)}, u32[]{:S(2)}) %all-to-all-start.5) | async-done | bytes 1900576 | tf_op jit(solution)/shard_map/all_to_all | solution.py:104
  389.1 0.2 fusion.45
  389.3 1.4 convolution_convert_fusion
  390.7 0.1 copy.56
  390.8 0.1 reshape.285
  390.9 0.7 copy.57
  (44 shorter events, 1.1 us)
Async XLA Ops:
  4.7 3.9 %copy-start.2 = (bf16[128,3584]{1,0:T(8,128)(2,1)S(1)}, bf16[128,3584]{1,0:T(8,128)(2,1)}, u32[]{:S(2)}) copy-start(bf16[128,3584]{1,0:T(8,128)(2,1)} %param.11) | copy-start | bytes 2752516
  62.3 1.8 copy-start
  73.0 78.2 %all-to-all-start.2 = ((bf16[32,24,3584]{2,1,0:T(8,128)(2,1)}), bf16[32,24,3584]{2,1,0:T(8,128)(2,1)}, u32[]{:S(2)}, u32[]{:S(2)}) async-start(bf16[32,24,3584]{2,1,0:T(8,128)(2,1)} %fusion.37), calls=%async_computation.2 | async-start | bytes 11010048 | tf_op jit(solution)/shard_map/all_to_all | solution.py:68
  151.3 81.1 %all-to-all-start.1 = ((bf16[32,24,3712]{2,1,0:T(8,128)(2,1)}), bf16[32,24,3712]{2,1,0:T(8,128)(2,1)}, u32[]{:S(2)}, u32[]{:S(2)}) async-start(bf16[32,24,3712]{2,1,0:T(8,128)(2,1)} %fusion.35), calls=%async_computation.1 | async-start | bytes 11403264 | tf_op jit(solution)/shard_map/all_to_all | solution.py:68
  232.3 11.0 %copy-start.7 = (f32[768,1024]{1,0:T(8,128)S(1)}, f32[768,1024]{1,0:T(8,128)}, u32[]{:S(2)}) copy-start(f32[768,1024]{1,0:T(8,128)} %fusion.2) | copy-start | bytes 9437188
  232.3 29.5 %slice-start = ((s8[7340032]{0:T(1024)(128)(4,1)}), s8[3145728]{0:T(1024)(128)(4,1)S(1)}, s32[]{:S(2)}) async-start(s8[7340032]{0:T(1024)(128)(4,1)} %bitcast.117), calls=%async_computation.6 | async-start | bytes 6291456
  243.4 18.5 %slice-start.1 = ((s8[7340032]{0:T(1024)(128)(4,1)}), s8[4194304]{0:T(1024)(128)(4,1)S(1)}, s32[]{:S(2)}) async-start(s8[7340032]{0:T(1024)(128)(4,1)} %bitcast.117), calls=%async_computation.7 | async-start | bytes 8388608
  255.6 6.2 %copy-start.3 = (bf16[768,1024]{1,0:T(8,128)(2,1)}, bf16[768,1024]{1,0:T(8,128)(2,1)S(1)}, u32[]{:S(2)}) copy-start(bf16[768,1024]{1,0:T(8,128)(2,1)S(1)} %get-tuple-element.39) | copy-start | bytes 4718596
  255.6 6.3 %copy-start.5 = (bf16[768,1024]{1,0:T(8,128)(2,1)}, bf16[768,1024]{1,0:T(8,128)(2,1)S(1)}, u32[]{:S(2)}) copy-start(bf16[768,1024]{1,0:T(8,128)(2,1)S(1)} %get-tuple-element.38) | copy-start | bytes 4718596
  266.3 45.8 %all-to-all-start.4 = ((bf16[32,24,1792]{2,1,0:T(8,128)(2,1)}), bf16[32,24,1792]{2,1,0:T(8,128)(2,1)S(1)}, u32[]{:S(2)}, u32[]{:S(2)}) async-start(bf16[32,24,1792]{2,1,0:T(8,128)(2,1)} %bitcast.111), calls=%async_computation.4 | async-start | bytes 5505024 | tf_op jit(solution)/shard_map/all_to_all | solution.py:68
  276.7 12.5 %copy-start.4 = (bf16[768,1024]{1,0:T(8,128)(2,1)S(1)}, bf16[768,1024]{1,0:T(8,128)(2,1)}, u32[]{:S(2)}) copy-start(bf16[768,1024]{1,0:T(8,128)(2,1)} %copy-done.3) | copy-start | bytes 4718596
  289.2 5.2 %copy-start.6 = (bf16[768,1024]{1,0:T(8,128)(2,1)S(1)}, bf16[768,1024]{1,0:T(8,128)(2,1)}, u32[]{:S(2)}) copy-start(bf16[768,1024]{1,0:T(8,128)(2,1)} %copy-done.5) | copy-start | bytes 4718596
  312.0 1.6 copy-start.1
  313.6 42.4 %all-to-all-start.3 = ((bf16[32,24,1920]{2,1,0:T(8,128)(2,1)}), bf16[32,24,1920]{2,1,0:T(8,128)(2,1)S(1)}, u32[]{:S(2)}, u32[]{:S(2)}) async-start(bf16[32,24,1920]{2,1,0:T(8,128)(2,1)} %bitcast.17), calls=%async_computation.3 | async-start | bytes 5898240 | tf_op jit(solution)/shard_map/all_to_all | solution.py:68
  362.0 27.1 %all-to-all-start.5 = ((bf16[4,64,3712]{2,1,0:T(8,128)(2,1)}), bf16[4,64,3712]{2,1,0:T(8,128)(2,1)S(1)}, u32[]{:S(2)}, u32[]{:S(2)}) async-start(bf16[4,64,3712]{2,1,0:T(8,128)(2,1)} %pad_maximum_fusion), calls=%async_computation.5 | async-start | bytes 3801088 | tf_op jit(solution)/shard_map/all_to_all | solution.py:104

commit v3 on v1

--- a/solution.py
+++ b/solution.py
@@ -16,7 +16,7 @@
     expert_count = group_count * local_count
     mean_pair = token_rows * top_count // expert_count
     pair_cap = mean_pair + (mean_pair + 1) // 2
-    slot_cap = (pair_cap + 7) // 8 * 8
+    slot_cap = pair_cap
     gate_mat = gate_weight[0]
     up_mat = up_weight[0]
     down_mat = down_weight[0]
@@ -44,9 +44,10 @@
     )
 
     def a2a(v):
-        v = v.reshape(expert_count, slot_cap, v.shape[-1])
+        width = v.shape[-1]
+        v = v.reshape(expert_count, slot_cap * width // lane, lane)
         v = lax.all_to_all(v, ("group", "local"), split_axis=0, concat_axis=0, tiled=True)
-        return v.reshape(slot_total, v.shape[-1])
+        return v.reshape(slot_total, width)
 
     rows_x = a2a(send_x)
     gate_pre = jnp.dot(rows_x, gate_mat, preferred_element_type=jnp.float32)

time: 362 us -> 335 us (0.925)
  waiting for transfers between devices: 200 us -> 126 us
  local copies, waits for them, and re-layouts: 12.3 us -> 83.4 us
  matrix products: 105 us -> 82.3 us
    all_to_all x4, waiting for transfers between devices: 200 us -> 126 us  [a2a(): lax.all_to_all(v, ('group', 'local'), split_axis=0, concat_axis=0, tiled=...]
    reshape x0 -> x8, local copies, waits for them, and re-layouts: none -> 71.2 us  [the longest x4 36.2 us: a2a(): v = v.reshape(expert_count, slot_cap * width // lane, lane)]
    dot_general x5, matrix products: 43.1 us -> 31.2 us  [_t_dot(): lax.dot_general(a, b, (((1,), (1,)), ((), ())), preferred_element_type=jn...]
  transfers between devices with their start and end apart: 4 -> 4, of which waited for: 4 -> 4; matrix products, arithmetic and copies ran while one was open for 22% -> 28% of each run, Pallas kernels for 0% -> 0%
where the time goes in v3:
time: 335 us; the launch traced here: 333 us
  waiting for transfers between devices  126 us (38%)
  local copies, waits for them, and re-layouts  83.4 us (25%)
  matrix products  82.3 us (25%)
  starting transfers between devices  33.4 us (10%)
  other arithmetic  7.29 us (2%)
    all_to_all x4, waiting for transfers between devices, a2a(): lax.all_to_all(v, ('group', 'local'), split_axis=0, concat_axis=0, tiled=...  126 us
    reshape x4, local copies, waits for them, and re-layouts, a2a(): v = v.reshape(expert_count, slot_cap * width // lane, lane)  36.2 us
    reshape x4, local copies, waits for them, and re-layouts, a2a(): return v.reshape(slot_total, width)  35 us
    all_to_all x4, starting transfers between devices, a2a(): lax.all_to_all(v, ('group', 'local'), split_axis=0, concat_axis=0, tiled=...  33.4 us
    dot_general x5, matrix products, _t_dot(): lax.dot_general(a, b, (((1,), (1,)), ((), ())), preferred_element_type=jn...  31.2 us
    dot_general x1, matrix products, local(): output = jnp.dot(hidden, down_mat, preferred_element_type=jnp.float32)  11.6 us
    dot_general x1, matrix products, local(): up_pre = jnp.dot(rows_x, up_mat, preferred_element_type=jnp.float32)  10.9 us
    dot_general x1, matrix products, local(): gate_pre = jnp.dot(rows_x, gate_mat, preferred_element_type=jnp.float32)  10.6 us
  transfers between devices with their start and end apart: 4, of which 4 were waited for; matrix products, arithmetic and copies ran while one was open for 28% of the time, Pallas kernels for 0%

profile of v3, /device:TPU:1, one launch (start us, length us, event | category | flops | bytes accessed | tf_op | source)
XLA Modules:
  0.0 333.2 jit_solution(13586491982219768508)
XLA Ops:
  0.6 0.0 copy-start
  0.6 0.9 copy.32
  1.5 0.1 eq.45
  1.6 0.1 eq.49
  1.7 0.1 copy.34
  1.8 0.2 fusion.46
  2.1 0.1 add_add_fusion
  2.2 0.2 fusion.45
  2.4 0.1 reduce_sum.21
  2.6 0.1 copy.36
  2.6 0.7 multiply_add_fusion.1
  3.3 0.2 fusion.41
  3.5 0.0 copy-done
  3.5 4.0 %fusion.55 = bf16[768,3584]{1,0:T(8,128)(2,1)} fusion(pred[768,128]{1,0:T(8,128)(4,1)S(1)} %fusion.41, bf16[128,3584]{1,0:T(8,128)(2,1)S(1)} %copy-done), kind=kOutput, calls=%fused_computation.72 | convolution fusion | flops 704643072 | bytes 6520832 | tf_op jit(solution)/shard_map/dot_general | solution.py:37
  7.5 11.2 %reshape.161 = bf16[128,168,128]{2,1,0:T(8,128)(2,1)} reshape(bf16[768,3584]{1,0:T(8,128)(2,1)} %fusion.55) | data formatting | bytes 11010048 | tf_op jit(solution)/shard_map/reshape | solution.py:48
  18.7 11.9 %all-to-all-start.1 = ((bf16[128,168,128]{2,1,0:T(8,128)(2,1)}), bf16[128,168,128]{2,1,0:T(8,128)(2,1)}, u32[]{:S(2)}, u32[]{:S(2)}) async-start(bf16[128,168,128]{2,1,0:T(8,128)(2,1)} %reshape.161), calls=%async_computation.1 | async-start | bytes 11010048 | tf_op jit(solution)/shard_map/all_to_all | solution.py:49
  30.6 0.6 compare_reduce_fusion
  31.2 0.0 copy-done.3
  31.2 0.6 broadcast_select_fusion
  31.9 0.1 copy.37
  32.0 0.1 reshape.170
  32.1 0.0 copy-done.2
  32.1 2.8 broadcast_in_dim.2
  34.9 6.7 %reshape.157 = bf16[512,3584]{1,0:T(8,128)(2,1)} reshape(bf16[128,4,3584]{2,1,0:T(4,128)(2,1)} %broadcast_in_dim.2) | data formatting | bytes 7340032 | tf_op jit(solution)/shard_map/reshape | solution.py:39
  41.7 7.8 %fusion.11 = bf16[768,3712]{1,0:T(8,128)(2,1)} fusion(bf16[512,1]{1,0:T(8,128)(2,1)S(1)} %reshape.170, bf16[512,3584]{1,0:T(8,128)(2,1)} %reshape.157, s32[512]{0:T(512)S(1)} %multiply_add_fusion), kind=kOutput, calls=%fused_computation.16 | convolution fusion | flops 2931032064 | bytes 9374720 | tf_op jit(solution)/shard_map/dot_general | solution.py:42
  49.5 11.9 %reshape.159 = bf16[128,174,128]{2,1,0:T(8,128)(2,1)} reshape(bf16[768,3712]{1,0:T(8,128)(2,1)} %fusion.11) | data formatting | bytes 11403264 | tf_op jit(solution)/shard_map/reshape | solution.py:48
  61.4 37.7 %all-to-all-done.1 = bf16[128,168,128]{2,1,0:T(8,128)(2,1)} async-done(((bf16[128,168,128]{2,1,0:T(8,128)(2,1)}), bf16[128,168,128]{2,1,0:T(8,128)(2,1)}, u32[]{:S(2)}, u32[]{:S(2)}) %all-to-all-start.1) | async-done | bytes 5505056 | tf_op jit(solution)/shard_map/all_to_all | solution.py:49
  99.1 7.8 %all-to-all-start = ((bf16[128,174,128]{2,1,0:T(8,128)(2,1)}), bf16[128,174,128]{2,1,0:T(8,128)(2,1)}, u32[]{:S(2)}, u32[]{:S(2)}) async-start(bf16[128,174,128]{2,1,0:T(8,128)(2,1)} %reshape.159), calls=%async_computation | async-start | bytes 11534336 | tf_op jit(solution)/shard_map/all_to_all | solution.py:49
  106.9 10.7 %reshape.162 = bf16[768,3584]{1,0:T(8,128)(2,1)} reshape(bf16[128,168,128]{2,1,0:T(8,128)(2,1)} %all-to-all-done.1) | data formatting | bytes 11010048 | tf_op jit(solution)/shard_map/reshape | solution.py:50
  117.5 10.9 %fusion.3 = f32[768,1024]{1,0:T(8,128)} fusion(bf16[768,3584]{1,0:T(8,128)(2,1)} %reshape.162, bf16[1,3584,1024]{2,1,0:T(8,128)(2,1)} %param.16), kind=kOutput, calls=%fused_computation.5 | convolution fusion | flops 5637144576 | bytes 15990784 | tf_op jit(solution)/shard_map/dot_general | solution.py:54
  128.5 48.9 %all-to-all-done = bf16[128,174,128]{2,1,0:T(8,128)(2,1)} async-done(((bf16[128,174,128]{2,1,0:T(8,128)(2,1)}), bf16[128,174,128]{2,1,0:T(8,128)(2,1)}, u32[]{:S(2)}, u32[]{:S(2)}) %all-to-all-start) | async-done | bytes 5701664 | tf_op jit(solution)/shard_map/all_to_all | solution.py:49
  177.4 11.6 %reshape.160 = bf16[768,3712]{1,0:T(8,128)(2,1)} reshape(bf16[128,174,128]{2,1,0:T(8,128)(2,1)} %all-to-all-done) | data formatting | bytes 11403264 | tf_op jit(solution)/shard_map/reshape | solution.py:50
  189.0 1.1 convert_reduce_fusion
  190.1 0.0 copy-start.8
  190.1 0.0 slice-start.2
  190.1 9.9 %fusion.6 = f32[768,1024]{1,0:T(8,128)S(1)} fusion(bf16[1,1024,3584]{2,1,0:T(8,128)(2,1)} %param.17, bf16[768,3712]{1,0:T(8,128)(2,1)} %reshape.160), kind=kOutput, calls=%fused_computation.8 | convolution fusion | flops 5637144576 | bytes 15990784 | tf_op jit(solution)/shard_map/dot_general | solution.py:8
  200.1 0.0 slice-done
  200.1 0.0 slice-done.1
  200.1 0.0 copy-done.8
  200.1 0.0 slice-start.3
  200.1 10.6 %multiply_convert_fusion.2 = (bf16[768,1024]{1,0:T(8,128)(2,1)S(1)}, bf16[768,1024]{1,0:T(8,128)(2,1)S(1)}, f32[768,1024]{1,0:T(8,128)}) fusion(f32[768,1024]{1,0:T(8,128)S(1)} %copy-done.8, f32[768,1024]{1,0:T(8,128)S(1)} %fusion.6, f32[768]{0:T(1024)S(1)} %convert_reduce_fusion, bf16[768,3584]{1,0:T(8,128)(2,1)S(1)} %bitcast.49, ...), kind=kOutput, calls=%fused_computation.34 | convolution fusion | flops 5648154624 | bytes 25431040 | tf_op jit(solution)/shard_map/dot_general | solution.py:53
  210.7 6.2 %fusion.16 = f32[768,1792]{1,0:T(8,128)S(1)} fusion(bf16[768,1024]{1,0:T(8,128)(2,1)S(1)} %get-tuple-element.35, bf16[1,3584,1024]{2,1,0:T(8,128)(2,1)} %param.16), kind=kOutput, calls=%fused_computation.20 | convolution fusion | flops 2818572288 | bytes 10747904 | tf_op jit(solution)/shard_map/dot_general | solution.py:8
  217.0 0.0 copy-done.4
  217.0 4.4 %add_convert_fusion = bf16[768,1792]{1,0:T(8,128)(2,1)} fusion(f32[768,1792]{1,0:T(8,128)S(1)} %fusion.16, bf16[768,1024]{1,0:T(8,128)(2,1)S(1)} %get-tuple-element.34, bf16[1,3584,1024]{2,1,0:T(8,128)(2,1)S(1)} %bitcast.51), kind=kOutput, calls=%fused_computation.12 | convolution fusion | flops 2821324800 | bytes 13500416 | tf_op jit(solution)/shard_map/dot_general | solution.py:8
  221.4 6.4 %reshape.166 = bf16[128,84,128]{2,1,0:T(8,128)(2,1)} reshape(bf16[768,1792]{1,0:T(8,128)(2,1)} %add_convert_fusion) | data formatting | bytes 5505024 | tf_op jit(solution)/shard_map/reshape | solution.py:48
  227.9 7.9 %all-to-all-start.3 = ((bf16[128,84,128]{2,1,0:T(8,128)(2,1)}), bf16[128,84,128]{2,1,0:T(8,128)(2,1)}, u32[]{:S(2)}, u32[]{:S(2)}) async-start(bf16[128,84,128]{2,1,0:T(8,128)(2,1)} %reshape.166), calls=%async_computation.3 | async-start | bytes 5767168 | tf_op jit(solution)/shard_map/all_to_all | solution.py:49
  235.7 11.6 %multiply_reduce_fusion = bf16[768]{0:T(1024)(128)(2,1)S(1)} fusion(bf16[1,1024,3584]{2,1,0:T(8,128)(2,1)} %param.17, bf16[768,3712]{1,0:T(8,128)(2,1)} %reshape.160, f32[768,1024]{1,0:T(8,128)} %fusion.3, f32[768,1024]{1,0:T(8,128)} %get-tuple-element.36), kind=kOutput, calls=%fused_computation | convolution fusion | flops 5650119680 | bytes 19138048 | tf_op jit(solution)/shard_map/dot_general | solution.py:58
  247.4 0.7 convert_select_fusion
  248.1 0.2 reshape.169
  248.2 5.2 %fusion.20 = f32[768,1792]{1,0:T(8,128)S(1)} fusion(bf16[768,1024]{1,0:T(8,128)(2,1)S(1)} %copy-done.5, bf16[1,3584,1024]{2,1,0:T(8,128)(2,1)} %param.16), kind=kOutput, calls=%fused_computation.24 | convolution fusion | flops 2818572288 | bytes 10747904 | tf_op jit(solution)/shard_map/dot_general | solution.py:8
  253.5 5.4 %add_convert_fusion.1 = bf16[768,1792]{1,0:T(8,128)(2,1)S(1)} fusion(f32[768,1792]{1,0:T(8,128)S(1)} %fusion.20, bf16[768,1024]{1,0:T(8,128)(2,1)S(1)} %copy-done.7, bf16[1,3584,1024]{2,1,0:T(8,128)(2,1)} %param.15), kind=kOutput, calls=%fused_computation.13 | convolution fusion | flops 2821324800 | bytes 13500416 | tf_op jit(solution)/shard_map/dot_general | solution.py:8
  258.9 1.8 fusion.33
  260.7 6.6 %reshape.164 = bf16[128,90,128]{2,1,0:T(8,128)(2,1)} reshape(bf16[768,1920]{1,0:T(8,128)(2,1)} %fusion.33) | data formatting | bytes 5898240 | tf_op jit(solution)/shard_map/reshape | solution.py:48
  267.4 6.6 %all-to-all-done.3 = bf16[128,84,128]{2,1,0:T(8,128)(2,1)} async-done(((bf16[128,84,128]{2,1,0:T(8,128)(2,1)}), bf16[128,84,128]{2,1,0:T(8,128)(2,1)}, u32[]{:S(2)}, u32[]{:S(2)}) %all-to-all-start.3) | async-done | bytes 2752544 | tf_op jit(solution)/shard_map/all_to_all | solution.py:49
  274.0 5.9 %all-to-all-start.2 = ((bf16[128,90,128]{2,1,0:T(8,128)(2,1)}), bf16[128,90,128]{2,1,0:T(8,128)(2,1)}, u32[]{:S(2)}, u32[]{:S(2)}) async-start(bf16[128,90,128]{2,1,0:T(8,128)(2,1)} %reshape.164), calls=%async_computation.2 | async-start | bytes 6291456 | tf_op jit(solution)/shard_map/all_to_all | solution.py:49
  279.9 6.2 %reshape.167 = bf16[768,1792]{1,0:T(8,128)(2,1)} reshape(bf16[128,84,128]{2,1,0:T(8,128)(2,1)} %all-to-all-done.3) | data formatting | bytes 5505024 | tf_op jit(solution)/shard_map/reshape | solution.py:50
  286.1 2.4 convolution_convert_fusion
  288.5 32.7 %all-to-all-done.2 = bf16[128,90,128]{2,1,0:T(8,128)(2,1)} async-done(((bf16[128,90,128]{2,1,0:T(8,128)(2,1)}), bf16[128,90,128]{2,1,0:T(8,128)(2,1)}, u32[]{:S(2)}, u32[]{:S(2)}) %all-to-all-start.2) | async-done | bytes 2949152 | tf_op jit(solution)/shard_map/all_to_all | solution.py:49
  321.1 6.4 %reshape.165 = bf16[768,1920]{1,0:T(8,128)(2,1)} reshape(bf16[128,90,128]{2,1,0:T(8,128)(2,1)} %all-to-all-done.2) | data formatting | bytes 5898240 | tf_op jit(solution)/shard_map/reshape | solution.py:50
  327.6 1.4 fusion.40
  329.0 2.4 fusion.36
  331.4 0.1 convert_element_type.50
  331.5 0.7 copy.40
  332.2 1.0 pad_maximum_fusion
  (23 shorter events, 0.1 us)
Async XLA Ops:
  0.6 2.9 copy-start
  18.7 12.6 %copy-start.3 = (bf16[128,4]{0,1:T(4,128)(2,1)S(1)}, bf16[128,4]{0,1:T(4,128)(2,1)}, u32[]{:S(2)}) copy-start(bf16[128,4]{0,1:T(4,128)(2,1)} %param.14) | copy-start | bytes 3076
  18.7 13.5 %copy-start.2 = (bf16[128,3584]{1,0:T(8,128)(2,1)S(1)}, bf16[128,3584]{1,0:T(8,128)(2,1)}, u32[]{:S(2)}) copy-start(bf16[128,3584]{1,0:T(8,128)(2,1)} %param.12) | copy-start | bytes 2752516
  18.7 80.4 %all-to-all-start.1 = ((bf16[128,168,128]{2,1,0:T(8,128)(2,1)}), bf16[128,168,128]{2,1,0:T(8,128)(2,1)}, u32[]{:S(2)}, u32[]{:S(2)}) async-start(bf16[128,168,128]{2,1,0:T(8,128)(2,1)} %reshape.161), calls=%async_computation.1 | async-start | bytes 11010048 | tf_op jit(solution)/shard_map/all_to_all | solution.py:49
  99.1 78.3 %all-to-all-start = ((bf16[128,174,128]{2,1,0:T(8,128)(2,1)}), bf16[128,174,128]{2,1,0:T(8,128)(2,1)}, u32[]{:S(2)}, u32[]{:S(2)}) async-start(bf16[128,174,128]{2,1,0:T(8,128)(2,1)} %reshape.159), calls=%async_computation | async-start | bytes 11534336 | tf_op jit(solution)/shard_map/all_to_all | solution.py:49
  177.4 22.7 %slice-start = ((s8[5505024]{0:T(1024)(128)(4,1)}), s8[1310720]{0:T(1024)(128)(4,1)S(1)}, s32[]{:S(2)}) async-start(s8[5505024]{0:T(1024)(128)(4,1)} %bitcast.48), calls=%async_computation.4 | async-start | bytes 2621440
  190.1 10.0 %slice-start.1 = ((s8[5505024]{0:T(1024)(128)(4,1)}), s8[4194304]{0:T(1024)(128)(4,1)S(1)}, s32[]{:S(2)}) async-start(s8[5505024]{0:T(1024)(128)(4,1)} %bitcast.48), calls=%async_computation.5 | async-start | bytes 8388608
  190.1 10.0 %copy-start.8 = (f32[768,1024]{1,0:T(8,128)S(1)}, f32[768,1024]{1,0:T(8,128)}, u32[]{:S(2)}) copy-start(f32[768,1024]{1,0:T(8,128)} %fusion.3) | copy-start | bytes 9437188
  190.1 26.9 %slice-start.2 = ((s8[7340032]{0:T(1024)(128)(4,1)}), s8[3145728]{0:T(1024)(128)(4,1)S(1)}, s32[]{:S(2)}) async-start(s8[7340032]{0:T(1024)(128)(4,1)} %bitcast.50), calls=%async_computation.6 | async-start | bytes 6291456
  200.1 16.9 %slice-start.3 = ((s8[7340032]{0:T(1024)(128)(4,1)}), s8[4194304]{0:T(1024)(128)(4,1)S(1)}, s32[]{:S(2)}) async-start(s8[7340032]{0:T(1024)(128)(4,1)} %bitcast.50), calls=%async_computation.7 | async-start | bytes 8388608
  210.7 6.2 %copy-start.4 = (bf16[768,1024]{1,0:T(8,128)(2,1)}, bf16[768,1024]{1,0:T(8,128)(2,1)S(1)}, u32[]{:S(2)}) copy-start(bf16[768,1024]{1,0:T(8,128)(2,1)S(1)} %get-tuple-element.35) | copy-start | bytes 4718596
  210.7 6.3 %copy-start.6 = (bf16[768,1024]{1,0:T(8,128)(2,1)}, bf16[768,1024]{1,0:T(8,128)(2,1)S(1)}, u32[]{:S(2)}) copy-start(bf16[768,1024]{1,0:T(8,128)(2,1)S(1)} %get-tuple-element.34) | copy-start | bytes 4718596
  227.9 46.1 %all-to-all-start.3 = ((bf16[128,84,128]{2,1,0:T(8,128)(2,1)}), bf16[128,84,128]{2,1,0:T(8,128)(2,1)}, u32[]{:S(2)}, u32[]{:S(2)}) async-start(bf16[128,84,128]{2,1,0:T(8,128)(2,1)} %reshape.166), calls=%async_computation.3 | async-start | bytes 5767168 | tf_op jit(solution)/shard_map/all_to_all | solution.py:49
  235.7 12.5 %copy-start.5 = (bf16[768,1024]{1,0:T(8,128)(2,1)S(1)}, bf16[768,1024]{1,0:T(8,128)(2,1)}, u32[]{:S(2)}) copy-start(bf16[768,1024]{1,0:T(8,128)(2,1)} %copy-done.4) | copy-start | bytes 4718596
  248.2 5.2 %copy-start.7 = (bf16[768,1024]{1,0:T(8,128)(2,1)S(1)}, bf16[768,1024]{1,0:T(8,128)(2,1)}, u32[]{:S(2)}) copy-start(bf16[768,1024]{1,0:T(8,128)(2,1)} %copy-done.6) | copy-start | bytes 4718596
  274.0 47.2 %all-to-all-start.2 = ((bf16[128,90,128]{2,1,0:T(8,128)(2,1)}), bf16[128,90,128]{2,1,0:T(8,128)(2,1)}, u32[]{:S(2)}, u32[]{:S(2)}) async-start(bf16[128,90,128]{2,1,0:T(8,128)(2,1)} %reshape.164), calls=%async_computation.2 | async-start | bytes 6291456 | tf_op jit(solution)/shard_map/all_to_all | solution.py:49
  327.6 5.6 %copy-start.1 = (bf16[128,3584]{1,0:T(8,128)(2,1)S(1)}, bf16[128,3584]{1,0:T(8,128)(2,1)}, u32[]{:S(2)}) copy-start(bf16[128,3584]{1,0:T(8,128)(2,1)} %param.11) | copy-start | bytes 2752516

commit v4 on v3

--- a/solution.py
+++ b/solution.py
@@ -68,7 +68,7 @@
     ).astype(jnp.bfloat16)
     grad_up = (back_hidden * active).astype(jnp.bfloat16)
 
-    half = model_width // 2
+    half = model_width // 4
     contrib_a = (_t_dot(grad_gate, gate_mat[:half]) + _t_dot(grad_up, up_mat[:half])).astype(
         jnp.bfloat16
     )

time: 335 us -> 340 us (1.015)
  waiting for transfers between devices: 126 us -> 133 us
  local copies, waits for them, and re-layouts: 83.4 us -> 78.3 us
  starting transfers between devices: 33.4 us -> 37.4 us
    all_to_all x4, waiting for transfers between devices: 126 us -> 133 us  [a2a(): lax.all_to_all(v, ('group', 'local'), split_axis=0, concat_axis=0, tiled=...]
    all_to_all x4, starting transfers between devices: 33.4 us -> 37.4 us  [a2a(): lax.all_to_all(v, ('group', 'local'), split_axis=0, concat_axis=0, tiled=...]
  transfers between devices with their start and end apart: 4 -> 4, of which waited for: 4 -> 3; matrix products, arithmetic and copies ran while one was open for 28% -> 25% of each run, Pallas kernels for 0% -> 0%
where the time goes in v4:
time: 340 us; the launch traced here: 338 us
  waiting for transfers between devices  133 us (39%)
  matrix products  82.6 us (24%)
  local copies, waits for them, and re-layouts  78.3 us (23%)
  starting transfers between devices  37.4 us (11%)
  other arithmetic  5.69 us (2%)
    all_to_all x4, waiting for transfers between devices, a2a(): lax.all_to_all(v, ('group', 'local'), split_axis=0, concat_axis=0, tiled=...  133 us
    all_to_all x4, starting transfers between devices, a2a(): lax.all_to_all(v, ('group', 'local'), split_axis=0, concat_axis=0, tiled=...  37.4 us
    reshape x4, local copies, waits for them, and re-layouts, a2a(): v = v.reshape(expert_count, slot_cap * width // lane, lane)  33.5 us
    dot_general x5, matrix products, _t_dot(): lax.dot_general(a, b, (((1,), (1,)), ((), ())), preferred_element_type=jn...  33.5 us
    reshape x4, local copies, waits for them, and re-layouts, a2a(): return v.reshape(slot_total, width)  32.6 us
    dot_general x1, matrix products, local(): output = jnp.dot(hidden, down_mat, preferred_element_type=jnp.float32)  10.9 us
    dot_general x1, matrix products, local(): up_pre = jnp.dot(rows_x, up_mat, preferred_element_type=jnp.float32)  10.9 us
    dot_general x1, matrix products, local(): gate_pre = jnp.dot(rows_x, gate_mat, preferred_element_type=jnp.float32)  9.47 us
  transfers between devices with their start and end apart: 4, of which 3 were waited for; matrix products, arithmetic and copies ran while one was open for 25% of the time, Pallas kernels for 0%

profile of v4, /device:TPU:1, one launch (start us, length us, event | category | flops | bytes accessed | tf_op | source)
XLA Modules:
  0.0 338.2 jit_solution(11688055093451391397)
XLA Ops:
  0.6 0.0 copy-start
  0.6 0.9 copy.32
  1.5 0.1 eq.45
  1.6 0.1 eq.49
  1.7 0.1 copy.34
  1.8 0.2 fusion.46
  2.1 0.1 add_add_fusion
  2.2 0.2 fusion.45
  2.4 0.1 reduce_sum.21
  2.6 0.1 copy.36
  2.6 0.7 multiply_add_fusion.1
  3.3 0.2 fusion.34
  3.5 0.0 copy-done
  3.5 4.0 %fusion.55 = bf16[768,3584]{1,0:T(8,128)(2,1)} fusion(pred[768,128]{1,0:T(8,128)(4,1)S(1)} %fusion.34, bf16[128,3584]{1,0:T(8,128)(2,1)S(1)} %copy-done), kind=kOutput, calls=%fused_computation.72 | convolution fusion | flops 704643072 | bytes 6520832 | tf_op jit(solution)/shard_map/dot_general | solution.py:37
  7.5 11.1 %reshape.161 = bf16[128,168,128]{2,1,0:T(8,128)(2,1)} reshape(bf16[768,3584]{1,0:T(8,128)(2,1)} %fusion.55) | data formatting | bytes 11010048 | tf_op jit(solution)/shard_map/reshape | solution.py:48
  18.6 11.9 %all-to-all-start.1 = ((bf16[128,168,128]{2,1,0:T(8,128)(2,1)}), bf16[128,168,128]{2,1,0:T(8,128)(2,1)}, u32[]{:S(2)}, u32[]{:S(2)}) async-start(bf16[128,168,128]{2,1,0:T(8,128)(2,1)} %reshape.161), calls=%async_computation.1 | async-start | bytes 11010048 | tf_op jit(solution)/shard_map/all_to_all | solution.py:49
  30.6 0.6 compare_reduce_fusion
  31.2 0.0 copy-done.4
  31.2 0.6 broadcast_select_fusion
  31.9 0.1 copy.37
  32.0 0.1 reshape.170
  32.1 0.0 copy-done.3
  32.1 2.8 broadcast_in_dim.2
  34.9 6.7 %reshape.157 = bf16[512,3584]{1,0:T(8,128)(2,1)} reshape(bf16[128,4,3584]{2,1,0:T(4,128)(2,1)} %broadcast_in_dim.2) | data formatting | bytes 7340032 | tf_op jit(solution)/shard_map/reshape | solution.py:39
  41.7 7.8 %fusion.18 = bf16[768,3712]{1,0:T(8,128)(2,1)} fusion(bf16[512,1]{1,0:T(8,128)(2,1)S(1)} %reshape.170, bf16[512,3584]{1,0:T(8,128)(2,1)} %reshape.157, s32[512]{0:T(512)S(1)} %multiply_add_fusion), kind=kOutput, calls=%fused_computation.19 | convolution fusion | flops 2931032064 | bytes 9374720 | tf_op jit(solution)/shard_map/dot_general | solution.py:42
  49.5 11.9 %reshape.159 = bf16[128,174,128]{2,1,0:T(8,128)(2,1)} reshape(bf16[768,3712]{1,0:T(8,128)(2,1)} %fusion.18) | data formatting | bytes 11403264 | tf_op jit(solution)/shard_map/reshape | solution.py:48
  61.4 37.7 %all-to-all-done.1 = bf16[128,168,128]{2,1,0:T(8,128)(2,1)} async-done(((bf16[128,168,128]{2,1,0:T(8,128)(2,1)}), bf16[128,168,128]{2,1,0:T(8,128)(2,1)}, u32[]{:S(2)}, u32[]{:S(2)}) %all-to-all-start.1) | async-done | bytes 5505056 | tf_op jit(solution)/shard_map/all_to_all | solution.py:49
  99.1 7.8 %all-to-all-start = ((bf16[128,174,128]{2,1,0:T(8,128)(2,1)}), bf16[128,174,128]{2,1,0:T(8,128)(2,1)}, u32[]{:S(2)}, u32[]{:S(2)}) async-start(bf16[128,174,128]{2,1,0:T(8,128)(2,1)} %reshape.159), calls=%async_computation | async-start | bytes 11534336 | tf_op jit(solution)/shard_map/all_to_all | solution.py:49
  106.8 10.7 %reshape.162 = bf16[768,3584]{1,0:T(8,128)(2,1)} reshape(bf16[128,168,128]{2,1,0:T(8,128)(2,1)} %all-to-all-done.1) | data formatting | bytes 11010048 | tf_op jit(solution)/shard_map/reshape | solution.py:50
  117.5 10.9 %fusion.3 = f32[768,1024]{1,0:T(8,128)} fusion(bf16[768,3584]{1,0:T(8,128)(2,1)} %reshape.162, bf16[1,3584,1024]{2,1,0:T(8,128)(2,1)} %param.16), kind=kOutput, calls=%fused_computation.6 | convolution fusion | flops 5637144576 | bytes 15990784 | tf_op jit(solution)/shard_map/dot_general | solution.py:54
  128.4 49.0 %all-to-all-done = bf16[128,174,128]{2,1,0:T(8,128)(2,1)} async-done(((bf16[128,174,128]{2,1,0:T(8,128)(2,1)}), bf16[128,174,128]{2,1,0:T(8,128)(2,1)}, u32[]{:S(2)}, u32[]{:S(2)}) %all-to-all-start) | async-done | bytes 5701664 | tf_op jit(solution)/shard_map/all_to_all | solution.py:49
  177.4 11.6 %reshape.160 = bf16[768,3712]{1,0:T(8,128)(2,1)} reshape(bf16[128,174,128]{2,1,0:T(8,128)(2,1)} %all-to-all-done) | data formatting | bytes 11403264 | tf_op jit(solution)/shard_map/reshape | solution.py:50
  189.0 1.1 convert_reduce_fusion
  190.1 0.0 copy-start.8
  190.1 9.9 %fusion.6 = f32[768,1024]{1,0:T(8,128)S(1)} fusion(bf16[1,1024,3584]{2,1,0:T(8,128)(2,1)} %param.17, bf16[768,3712]{1,0:T(8,128)(2,1)} %reshape.160), kind=kOutput, calls=%fused_computation.9 | convolution fusion | flops 5637144576 | bytes 15990784 | tf_op jit(solution)/shard_map/dot_general | solution.py:8
  200.0 0.0 slice-done
  200.0 0.0 slice-done.1
  200.0 0.0 copy-done.8
  200.0 0.0 copy-start.2
  200.1 9.5 %multiply_convert_fusion.2 = (bf16[768,1024]{1,0:T(8,128)(2,1)S(1)}, bf16[768,1024]{1,0:T(8,128)(2,1)S(1)}, f32[768,1024]{1,0:T(8,128)S(1)}) fusion(f32[768,1024]{1,0:T(8,128)S(1)} %copy-done.8, f32[768,1024]{1,0:T(8,128)S(1)} %fusion.6, f32[768]{0:T(1024)S(1)} %convert_reduce_fusion, bf16[768,3584]{1,0:T(8,128)(2,1)S(1)} %bitcast.49, ...), kind=kOutput, calls=%fused_computation.27 | convolution fusion | flops 5648154624 | bytes 25431040 | tf_op jit(solution)/shard_map/dot_general | solution.py:53
  209.6 10.9 %multiply_reduce_fusion = bf16[768]{0:T(1024)(128)(2,1)S(1)} fusion(bf16[1,1024,3584]{2,1,0:T(8,128)(2,1)} %param.17, bf16[768,3712]{1,0:T(8,128)(2,1)S(1)} %copy-done.2, f32[768,1024]{1,0:T(8,128)S(1)} %copy-done.8, f32[768,1024]{1,0:T(8,128)S(1)} %get-tuple-element.36), kind=kOutput, calls=%fused_computation | convolution fusion | flops 5650119680 | bytes 19138048 | tf_op jit(solution)/shard_map/dot_general | solution.py:58
  220.5 0.7 convert_select_fusion
  221.2 0.2 reshape.169
  221.4 0.0 copy-done.7
  221.4 3.4 fusion.26
  224.7 3.4 %add_convert_fusion.1 = bf16[768,896]{1,0:T(8,128)(2,1)S(1)} fusion(f32[768,896]{1,0:T(8,128)S(1)} %fusion.26, bf16[768,1024]{1,0:T(8,128)(2,1)S(1)} %get-tuple-element.34, bf16[1,3584,1024]{2,1,0:T(8,128)(2,1)} %param.15), kind=kOutput, calls=%fused_computation.31 | convolution fusion | flops 1410662400 | bytes 7536640 | tf_op jit(solution)/shard_map/dot_general | solution.py:8
  228.2 0.2 fusion.32
  228.4 2.1 reshape.164
  230.5 7.5 %all-to-all-start.2 = ((bf16[128,48,128]{2,1,0:T(8,128)(2,1)}), bf16[128,48,128]{2,1,0:T(8,128)(2,1)S(1)}, u32[]{:S(2)}, u32[]{:S(2)}) async-start(bf16[128,48,128]{2,1,0:T(8,128)(2,1)} %reshape.164), calls=%async_computation.2 | async-start | bytes 3145728 | tf_op jit(solution)/shard_map/all_to_all | solution.py:49
  238.0 7.8 %fusion.8 = f32[768,2688]{1,0:T(8,128)S(1)} fusion(bf16[768,1024]{1,0:T(8,128)(2,1)} %copy-done.7, bf16[1,3584,1024]{2,1,0:T(8,128)(2,1)} %param.16), kind=kOutput, calls=%fused_computation.11 | convolution fusion | flops 4227858432 | bytes 15335424 | tf_op jit(solution)/shard_map/dot_general | solution.py:8
  245.8 0.0 copy-done.6
  245.8 9.0 %add_convert_fusion = bf16[768,2688]{1,0:T(8,128)(2,1)} fusion(f32[768,2688]{1,0:T(8,128)S(1)} %fusion.8, bf16[768,1024]{1,0:T(8,128)(2,1)S(1)} %copy-done.6, bf16[1,3584,1024]{2,1,0:T(8,128)(2,1)} %param.15), kind=kOutput, calls=%fused_computation.1 | convolution fusion | flops 4231987200 | bytes 19464192 | tf_op jit(solution)/shard_map/dot_general | solution.py:8
  254.8 8.3 %reshape.166 = bf16[128,126,128]{2,1,0:T(8,128)(2,1)} reshape(bf16[768,2688]{1,0:T(8,128)(2,1)} %add_convert_fusion) | data formatting | bytes 8257536 | tf_op jit(solution)/shard_map/reshape | solution.py:48
  263.2 0.0 all-to-all-done.2
  263.2 10.2 %all-to-all-start.3 = ((bf16[128,126,128]{2,1,0:T(8,128)(2,1)}), bf16[128,126,128]{2,1,0:T(8,128)(2,1)}, u32[]{:S(2)}, u32[]{:S(2)}) async-start(bf16[128,126,128]{2,1,0:T(8,128)(2,1)} %reshape.166), calls=%async_computation.3 | async-start | bytes 8388608 | tf_op jit(solution)/shard_map/all_to_all | solution.py:49
  273.4 2.1 reshape.165
  275.5 1.3 fusion.33
  276.9 0.1 convert_element_type.50
  277.0 0.7 copy.40
  277.7 1.8 fusion.39
  279.5 46.6 %all-to-all-done.3 = bf16[128,126,128]{2,1,0:T(8,128)(2,1)} async-done(((bf16[128,126,128]{2,1,0:T(8,128)(2,1)}), bf16[128,126,128]{2,1,0:T(8,128)(2,1)}, u32[]{:S(2)}, u32[]{:S(2)}) %all-to-all-start.3) | async-done | bytes 4128800 | tf_op jit(solution)/shard_map/all_to_all | solution.py:49
  326.0 8.2 %reshape.167 = bf16[768,2688]{1,0:T(8,128)(2,1)} reshape(bf16[128,126,128]{2,1,0:T(8,128)(2,1)} %all-to-all-done.3) | data formatting | bytes 8257536 | tf_op jit(solution)/shard_map/reshape | solution.py:50
  334.2 3.0 convolution_convert_fusion
  337.2 1.0 pad_maximum_fusion
  (18 shorter events, 0.1 us)
Async XLA Ops:
  0.6 2.9 copy-start
  18.6 12.6 %copy-start.4 = (bf16[128,4]{0,1:T(4,128)(2,1)S(1)}, bf16[128,4]{0,1:T(4,128)(2,1)}, u32[]{:S(2)}) copy-start(bf16[128,4]{0,1:T(4,128)(2,1)} %param.14) | copy-start | bytes 3076
  18.6 13.5 %copy-start.3 = (bf16[128,3584]{1,0:T(8,128)(2,1)S(1)}, bf16[128,3584]{1,0:T(8,128)(2,1)}, u32[]{:S(2)}) copy-start(bf16[128,3584]{1,0:T(8,128)(2,1)} %param.12) | copy-start | bytes 2752516
  18.6 80.4 %all-to-all-start.1 = ((bf16[128,168,128]{2,1,0:T(8,128)(2,1)}), bf16[128,168,128]{2,1,0:T(8,128)(2,1)}, u32[]{:S(2)}, u32[]{:S(2)}) async-start(bf16[128,168,128]{2,1,0:T(8,128)(2,1)} %reshape.161), calls=%async_computation.1 | async-start | bytes 11010048 | tf_op jit(solution)/shard_map/all_to_all | solution.py:49
  99.1 78.3 %all-to-all-start = ((bf16[128,174,128]{2,1,0:T(8,128)(2,1)}), bf16[128,174,128]{2,1,0:T(8,128)(2,1)}, u32[]{:S(2)}, u32[]{:S(2)}) async-start(bf16[128,174,128]{2,1,0:T(8,128)(2,1)} %reshape.159), calls=%async_computation | async-start | bytes 11534336 | tf_op jit(solution)/shard_map/all_to_all | solution.py:49
  177.4 22.6 %slice-start = ((s8[5505024]{0:T(1024)(128)(4,1)}), s8[1310720]{0:T(1024)(128)(4,1)S(1)}, s32[]{:S(2)}) async-start(s8[5505024]{0:T(1024)(128)(4,1)} %bitcast.48), calls=%async_computation.4 | async-start | bytes 2621440
  190.1 10.0 %slice-start.1 = ((s8[5505024]{0:T(1024)(128)(4,1)}), s8[4194304]{0:T(1024)(128)(4,1)S(1)}, s32[]{:S(2)}) async-start(s8[5505024]{0:T(1024)(128)(4,1)} %bitcast.48), calls=%async_computation.5 | async-start | bytes 8388608
  190.1 10.0 %copy-start.8 = (f32[768,1024]{1,0:T(8,128)S(1)}, f32[768,1024]{1,0:T(8,128)}, u32[]{:S(2)}) copy-start(f32[768,1024]{1,0:T(8,128)} %fusion.3) | copy-start | bytes 9437188
  200.0 9.5 %copy-start.2 = (bf16[768,3712]{1,0:T(8,128)(2,1)S(1)}, bf16[768,3712]{1,0:T(8,128)(2,1)}, u32[]{:S(2)}) copy-start(bf16[768,3712]{1,0:T(8,128)(2,1)} %reshape.160) | copy-start | bytes 17104900
  209.5 11.8 %copy-start.7 = (bf16[768,1024]{1,0:T(8,128)(2,1)}, bf16[768,1024]{1,0:T(8,128)(2,1)S(1)}, u32[]{:S(2)}) copy-start(bf16[768,1024]{1,0:T(8,128)(2,1)S(1)} %get-tuple-element.35) | copy-start | bytes 4718596
  209.5 15.2 %copy-start.5 = (bf16[768,1024]{1,0:T(8,128)(2,1)}, bf16[768,1024]{1,0:T(8,128)(2,1)S(1)}, u32[]{:S(2)}) copy-start(bf16[768,1024]{1,0:T(8,128)(2,1)S(1)} %get-tuple-element.34) | copy-start | bytes 4718596
  230.5 32.7 %all-to-all-start.2 = ((bf16[128,48,128]{2,1,0:T(8,128)(2,1)}), bf16[128,48,128]{2,1,0:T(8,128)(2,1)S(1)}, u32[]{:S(2)}, u32[]{:S(2)}) async-start(bf16[128,48,128]{2,1,0:T(8,128)(2,1)} %reshape.164), calls=%async_computation.2 | async-start | bytes 3145728 | tf_op jit(solution)/shard_map/all_to_all | solution.py:49
  238.0 7.8 %copy-start.6 = (bf16[768,1024]{1,0:T(8,128)(2,1)S(1)}, bf16[768,1024]{1,0:T(8,128)(2,1)}, u32[]{:S(2)}) copy-start(bf16[768,1024]{1,0:T(8,128)(2,1)} %copy-done.5) | copy-start | bytes 4718596
  263.2 62.8 %all-to-all-start.3 = ((bf16[128,126,128]{2,1,0:T(8,128)(2,1)}), bf16[128,126,128]{2,1,0:T(8,128)(2,1)}, u32[]{:S(2)}, u32[]{:S(2)}) async-start(bf16[128,126,128]{2,1,0:T(8,128)(2,1)} %reshape.166), calls=%async_computation.3 | async-start | bytes 8388608 | tf_op jit(solution)/shard_map/all_to_all | solution.py:49
  326.0 12.2 %copy-start.1 = (bf16[128,3584]{1,0:T(8,128)(2,1)S(1)}, bf16[128,3584]{1,0:T(8,128)(2,1)}, u32[]{:S(2)}) copy-start(bf16[128,3584]{1,0:T(8,128)(2,1)} %param.11) | copy-start | bytes 2752516
